TPU v7x, 256 devices: a whole 4x4x8 slice. The times are simulated.
256 devices in a mesh: dp: 32 (over x, z_lo, core), fsdp: 8 (over y, z_hi).
Axes of the slice: x: 4, y: 4, z: 8 (z_hi: 2, z_lo: 4; z = z_hi * 4 + z_lo), core: 2. Of those that a mesh axis runs over, the one named last changes fastest.
Arguments:
- stream_rows: bfloat16 [16384, 4096], P(('dp', 'fsdp')), may hold values from -6 to 6
- ln_gain: float32 [4096], replicated, may hold values from 0.1 to 1.9
- ln_bias: float32 [4096], replicated, may hold values from -2 to 2
- w_q: bfloat16 [4096, 2048], P(None, 'fsdp')
- w_k: bfloat16 [4096, 2048], P(None, 'fsdp')
- w_v: bfloat16 [4096, 2048], P(None, 'fsdp'), may hold values from -0.09375 to 0.09375
- w_o: bfloat16 [2048, 4096], P('fsdp'), may hold values from -0.1875 to 0.1875
- scale_ls: float32 [4096], P('fsdp'), may hold values from 0.5 to 2
- sides: int32 [32, 1], P('dp'), may hold values from 10 to 18, as said below
- offsets: int32 [32, 1], P('dp'), may hold values from 0 to 0, as said below
- owners: int32 [32, 1], replicated, may hold values from 0 to 31, as said below
Outputs:
- delivered: bfloat16 [32, 1, 81, 4, 4096], P('dp', None, None, None, 'fsdp')
Inputs may be any that keep to these rules, and one draw needn't show every extreme that they name: `sides`: every side is even, and some image has side 18 in every draw. `offsets`: within a group the images lie back to back in index order from row 0, each taking 5 + side * side rows; the rows after the last image are padding. owners[g, j] = (g + c_j) mod 32, with offsets c_j that differ between image indices j; so the images of one group have different owners and every owner receives exactly one image of each index j.
All inputs are finite; a program needn't handle non-finite values.
Results may differ from a plain program's by a relative error of at most 0.012.
Values may be sent and summed in bfloat16 or wider, within the bound.
No kernel may reach another device: no remote copies, remote signals or barrier semaphores. Data moves between devices by JAX's collectives and lax.ppermute only.
A program may use at most 128 MiB of HBM per device.

v0:
```python
import math

import jax
import jax.numpy as jnp
import numpy as np
from jax import lax
from jax.sharding import Mesh
from jax.sharding import PartitionSpec as P

HEAD = 128
EXTRA = 5
CAP = 81
LIVE_ROWS = 336
MERGE_PAD = 328

norm_eps = 1e-06

DP_AXES = ("x", "zl", "c")
FSDP_AXES = ("y", "zh")


def layer_norm(raw_rows, ln_gain, ln_bias):
    values = raw_rows.astype(jnp.float32)
    centre = jnp.mean(values, axis=-1, keepdims=True)
    spread = jnp.mean(jnp.square(values - centre), axis=-1, keepdims=True)
    return ((values - centre) * lax.rsqrt(spread + norm_eps) * ln_gain + ln_bias).astype(
        jnp.bfloat16
    )


def row_layout(side_row, offset_row, count):
    row_ids = jnp.arange(count, dtype=jnp.int32)
    lengths = EXTRA + side_row * side_row
    inside = (
        (row_ids[:, None] >= offset_row[None, :])
        & (row_ids[:, None] < (offset_row + lengths)[None, :])
    ).astype(jnp.int32)
    covered = jnp.sum(inside, axis=1)
    image_ids = jnp.arange(side_row.shape[0], dtype=jnp.int32)
    segment = jnp.sum(inside * image_ids[None, :], axis=1) + (1 - covered) * side_row.shape[0]
    first_row = jnp.sum(inside * offset_row[None, :], axis=1)
    side_len = jnp.sum(inside * side_row[None, :], axis=1) + (1 - covered)
    patch_id = row_ids - first_row - EXTRA
    is_patch = (covered == 1) & (patch_id >= 0)
    clipped = jnp.maximum(patch_id, 0)
    across = clipped // side_len
    along = clipped % side_len
    side_float = side_len.astype(jnp.float32)
    coord_one = jnp.where(
        is_patch,
        (2 * across + 1).astype(jnp.float32) / side_float - 1.0,
        jnp.zeros_like(side_float),
    )
    coord_two = jnp.where(
        is_patch, (2 * along + 1).astype(jnp.float32) / side_float - 1.0, jnp.zeros_like(side_float)
    )
    return (segment, coord_one, coord_two)


def rotary_tables(coord_one, coord_two, head_size):
    dims = jnp.arange(head_size, dtype=jnp.int32)
    first_half = dims < head_size // 2
    freq_index = (dims % (head_size // 4)).astype(jnp.float32)
    rates = 3.0 * jnp.power(jnp.ones_like(freq_index) * 1.2, freq_index)
    coords = jnp.where(first_half[None, :], coord_one[:, None], coord_two[:, None])
    angles = coords * rates[None, :]
    return (jnp.cos(angles), jnp.sin(angles))


def rotate(tensor, cosine, sine_tab):
    row_count, head_count, head_size = tensor.shape
    quarters = tensor.reshape(row_count, head_count, 2, 2, head_size // 4)
    turned = jnp.stack([-quarters[:, :, :, 1], quarters[:, :, :, 0]], axis=3).reshape(tensor.shape)
    return tensor * cosine[:, None, :] + turned * sine_tab[:, None, :]


def softmax_rounded(scores):
    top = jnp.max(scores, axis=-1, keepdims=True)
    expo = jnp.exp(scores - top)
    return (expo / jnp.sum(expo, axis=-1, keepdims=True)).astype(jnp.bfloat16)


def merge_rows(side_len, offset):
    slot = jnp.arange(CAP, dtype=jnp.int32)
    half_side = side_len // 2
    across = slot // half_side
    along = slot % half_side
    valid = slot < half_side * half_side
    corner = jnp.arange(4, dtype=jnp.int32)
    source_rows = (
        offset
        + EXTRA
        + (2 * across[:, None] + corner[None, :] // 2) * side_len
        + 2 * along[:, None]
        + corner[None, :] % 2
    )
    source_rows = jnp.where(valid[:, None], source_rows, jnp.zeros_like(source_rows))
    return source_rows.reshape(CAP * 4), valid


def attention(queries, key_rows, value_rows, segment):
    scores = jnp.einsum(
        "qhd,khd->hqk", queries, key_rows, preferred_element_type=jnp.float32
    ) / math.sqrt(HEAD)
    allowed = segment[None, :, None] == segment[None, None, :]
    scores = jnp.where(allowed, scores, jnp.full_like(scores, -1e30))
    weights = softmax_rounded(scores)
    return jnp.einsum(
        "hqk,khd->qhd", weights, value_rows, preferred_element_type=jnp.float32
    ).astype(jnp.bfloat16)


def one_hot(rows, count):
    return (rows[:, None] == jnp.arange(count, dtype=jnp.int32)[None, :]).astype(jnp.bfloat16)


def swap_pair(array):
    return lax.ppermute(array, "zh", [(0, 1), (1, 0)])


def shift_dp(block, distance):
    count = 1
    for name in DP_AXES:
        count *= lax.axis_size(name)

    def branch(by):
        if by == 0:
            return lambda v: v
        pairs = [(i, (i + by) % count) for i in range(count)]
        return lambda v: lax.ppermute(v, DP_AXES, pairs)

    return lax.switch(distance, [branch(by) for by in range(count)], block)


def shift_by_exchange(payload, distance, count):
    size = payload.size
    lanes = 128
    rows = -(-size // (count * lanes))
    rows = -(-rows // 16) * 16
    flat = jnp.pad(payload.reshape(-1), (0, count * rows * lanes - size))
    pieces = lax.all_to_all(flat.reshape(count, rows, lanes), DP_AXES, 0, 0, tiled=True)
    rolled = jnp.roll(pieces, distance, axis=0)
    back = lax.all_to_all(rolled, DP_AXES, 0, 0, tiled=True)
    return back.reshape(-1)[:size].reshape(payload.shape)


def deliver_halves(mine, theirs, distance):
    count = 1
    for name in DP_AXES:
        count *= lax.axis_size(name)

    def branch(by):
        if by == 0:
            return lambda a, b: (a, swap_pair(b))
        same = [(i, (i + by) % count) for i in range(count)]
        across = [
            (2 * i + h, 2 * ((i + by) % count) + 1 - h) for i in range(count) for h in range(2)
        ]
        return lambda a, b: (
            lax.ppermute(a, DP_AXES, same),
            lax.ppermute(b, DP_AXES + ("zh",), across),
        )

    return lax.switch(distance, [branch(by) for by in range(count)], mine, theirs)


def body(stream_rows, ln_gain, ln_bias, w_q, w_k, w_v, w_o, scale_ls, sides, offsets, owners):
    head_cols = w_q.shape[1]
    local_heads = head_cols // HEAD
    side_row = sides[0]
    offset_row = offsets[0]
    feat_cols = scale_ls.shape[0]

    zh = lax.axis_index("zh")
    own_blocks = lax.all_gather(stream_rows, "y", axis=0, tiled=False)
    partner_blocks = lax.all_gather(swap_pair(stream_rows), "y", axis=0, tiled=False)
    live_rows = jnp.where(
        zh == 0,
        jnp.stack([own_blocks, partner_blocks], axis=1),
        jnp.stack([partner_blocks, own_blocks], axis=1),
    ).reshape(-1, stream_rows.shape[1])[:LIVE_ROWS]
    normed = layer_norm(live_rows, ln_gain, ln_bias)

    projected = jnp.concatenate(
        [
            jnp.dot(normed, w_q, preferred_element_type=jnp.float32),
            jnp.dot(normed, w_k, preferred_element_type=jnp.float32),
            jnp.dot(normed, w_v, preferred_element_type=jnp.float32),
        ],
        axis=1,
    )
    segment, coord_one, coord_two = row_layout(side_row, offset_row, LIVE_ROWS)
    cosine, sine_tab = rotary_tables(coord_one, coord_two, HEAD)
    queries = rotate(
        projected[:, :head_cols].reshape(LIVE_ROWS, local_heads, HEAD), cosine, sine_tab
    ).astype(jnp.bfloat16)
    key_rows = rotate(
        projected[:, head_cols : 2 * head_cols].reshape(LIVE_ROWS, local_heads, HEAD),
        cosine,
        sine_tab,
    ).astype(jnp.bfloat16)
    value_rows = (
        projected[:, 2 * head_cols :].astype(jnp.bfloat16).reshape(LIVE_ROWS, local_heads, HEAD)
    )
    attended = attention(queries, key_rows, value_rows, segment).reshape(LIVE_ROWS, head_cols)

    source_rows, valid = merge_rows(side_row[0], offset_row[0])
    padded_rows = jnp.concatenate(
        [source_rows, jnp.zeros((MERGE_PAD - source_rows.shape[0],), jnp.int32)]
    )
    merged_attended = jnp.dot(
        one_hot(padded_rows, LIVE_ROWS), attended, preferred_element_type=jnp.float32
    ).astype(jnp.bfloat16)
    partial_sum = jnp.dot(merged_attended, w_o, preferred_element_type=jnp.float32).astype(
        jnp.bfloat16
    )
    group_count = 1
    for name in DP_AXES:
        group_count *= lax.axis_size(name)
    distance = owners[0, 0] % group_count

    feat_index = lax.axis_index("y") * lax.axis_size("zh") + zh
    residual = jnp.dot(
        one_hot(source_rows, LIVE_ROWS),
        lax.dynamic_slice_in_dim(live_rows, feat_index * feat_cols, feat_cols, axis=1),
        preferred_element_type=jnp.float32,
    )

    quarter = lax.psum_scatter(partial_sum, "y", scatter_dimension=1, tiled=True)
    split = quarter.reshape(MERGE_PAD, 2, feat_cols)[: source_rows.shape[0]]
    mine = jnp.where(zh == 0, split[:, 0], split[:, 1])
    theirs = jnp.where(zh == 0, split[:, 1], split[:, 0])
    branch = mine.astype(jnp.float32) + swap_pair(theirs).astype(jnp.float32)
    updated = (residual + scale_ls * branch).astype(jnp.bfloat16)
    merged = jnp.where(jnp.repeat(valid, 4)[:, None], updated, jnp.zeros_like(updated))
    delivered = shift_by_exchange(merged, distance, group_count).reshape(
        1, CAP, 4, feat_cols
    )
    return delivered[None]


def solution(mesh):
    dp_size, fsdp_size = mesh.devices.shape
    split_mesh = Mesh(
        np.asarray(mesh.devices).reshape(4, dp_size // 8, 2, fsdp_size // 2, 2),
        DP_AXES + FSDP_AXES,
    )
    rows = DP_AXES + FSDP_AXES
    return jax.shard_map(
        body,
        mesh=split_mesh,
        in_specs=(
            P(rows, None),
            P(),
            P(),
            P(None, FSDP_AXES),
            P(None, FSDP_AXES),
            P(None, FSDP_AXES),
            P(FSDP_AXES, None),
            P(FSDP_AXES),
            P(DP_AXES, None),
            P(DP_AXES, None),
            P(),
        ),
        out_specs=P(DP_AXES, None, None, None, FSDP_AXES),
        check_vma=False,
    )
```

profile of v0, /device:TPU:1, one launch (start us, length us, event | category | flops | bytes accessed | tf_op | source)
XLA Modules:
  0.0 210.4 jit_solution(16921086275070443458)
XLA Ops:
  6.5 0.7 all-gather.5.cloned.1.call-update
  7.3 7.8 %collective-permute-start = (bf16[64,4096]{1,0:T(8,128)(2,1)}, bf16[64,4096]{1,0:T(8,128)(2,1)S(1)}, u32[]{:S(2)}, u32[]{:S(2)}) collective-permute-start(bf16[64,4096]{1,0:T(8,128)(2,1)} %param.11), channel_id=1, source_target_pairs={{0,1},{1,0},{2,3},{3,2},{4,5},{5,4},{6,7},{7,6},{8,9},{9,8},{10,11... | collective-permute-start | bytes 1572872 | tf_op jit(solution)/shard_map/ppermute | solution.py:118
  15.1 13.5 %collective-permute-done = bf16[64,4096]{1,0:T(8,128)(2,1)S(1)} collective-permute-done((bf16[64,4096]{1,0:T(8,128)(2,1)}, bf16[64,4096]{1,0:T(8,128)(2,1)S(1)}, u32[]{:S(2)}, u32[]{:S(2)}) %collective-permute-start) | collective-permute-done | bytes 524320 | tf_op jit(solution)/shard_map/ppermute | solution.py:118
  28.6 0.8 copy-done.4
  31.8 0.8 fusion.27
  32.6 13.5 %all-gather.5.cloned.1.call-done = bf16[256,4096]{1,0:T(8,128)(2,1)} async-done(((bf16[64,4096]{1,0:T(8,128)(2,1)}), bf16[256,4096]{1,0:T(8,128)(2,1)}) %all-gather.5.cloned.1.call-update) | async-done | bytes 2097168 | tf_op jit(solution)/shard_map/all_gather | solution.py:175
  46.1 35.2 %all-gather.7.cloned.1.call-done = bf16[256,4096]{1,0:T(8,128)(2,1)} async-done(((bf16[64,4096]{1,0:T(8,128)(2,1)}), bf16[256,4096]{1,0:T(8,128)(2,1)}) %all-gather.7.cloned.1.call-update) | async-done | bytes 2097168 | tf_op jit(solution)/shard_map/all_gather | solution.py:176
  81.4 4.3 %maximum_select_fusion = bf16[4,2,64,4096]{3,2,1,0:T(8,128)(2,1)S(1)} fusion(bf16[4,1,64,4096]{3,2,1,0:T(8,128)(2,1)} %bitcast.66, bf16[4,1,64,4096]{3,2,1,0:T(8,128)(2,1)} %bitcast.65, pred[]{:T(512)S(6)} %eq.84), kind=kLoop, calls=%fused_computation.10 | loop fusion | flops 6291456 | bytes 8388609 | tf_op jit(solution)/shard_map/jit(_where)/select_n | solution.py:177
  85.7 0.5 convert_reduce_fusion
  86.2 0.9 fusion.3
  87.0 0.6 copy-done.1
  87.6 1.4 fusion.6
  89.2 1.3 fusion.60
  90.6 0.2 copy-done.9
  90.8 1.3 fusion.59
  92.4 0.9 fusion.10
  93.5 1.5 fusion.58
  95.0 1.6 fusion.11
  96.6 2.8 %convolution_convert_fusion = bf16[328,4096]{1,0:T(8,128)(2,1)} fusion(bf16[256,4096]{1,0:T(8,128)(2,1)S(1)} %copy-done, s32[328]{0:T(512)S(1)} %concatenate.7, bf16[2,42,8,128]{3,2,1,0:T(8,128)(2,1)S(1)} %fusion.11), kind=kOutput, calls=%fused_computation.9 | convolution fusion | flops 745830016 | bytes 4957472 | tf_op jit(solution)/shard_map/dot_general | solution.py:214
  99.4 37.4 %reduce-scatter.2.cloned.1.call-done = bf16[328,1024]{1,0:T(8,128)(2,1)} async-done(((bf16[328,4096]{1,0:T(8,128)(2,1)}), bf16[328,1024]{1,0:T(8,128)(2,1)}) %reduce-scatter.2.cloned.1.call-update) | async-done | bytes 671760 | tf_op jit(solution)/shard_map/reduce_scatter | solution.py:229
  136.8 2.3 %slice.42 = bf16[324,2,512]{2,1,0:T(2,128)(2,1)S(1)} reshape(bf16[324,1024]{1,0:T(8,128)(2,1)} %bitcast.71) | data formatting | bytes 1327104 | tf_op jit(solution)/shard_map/slice | solution.py:230
  139.1 0.9 fusion.57
  140.0 0.8 copy-done.2
  141.0 5.5 %collective-permute-start.1 = (bf16[324,512]{1,0:T(8,128)(2,1)S(1)}, bf16[324,512]{1,0:T(8,128)(2,1)}, u32[]{:S(2)}, u32[]{:S(2)}) collective-permute-start(bf16[324,512]{1,0:T(8,128)(2,1)S(1)} %select_bitcast_fusion), channel_id=1, source_target_pairs={{0,1},{1,0},{2,3},{3,2},{4,5},{5,4},{6,7},{7,6},{8,9},{9,8},{10,11... | collective-permute-start | bytes 995336 | tf_op jit(solution)/shard_map/ppermute | solution.py:118
  146.5 2.0 slice.47
  148.5 7.1 %collective-permute-done.1 = bf16[324,512]{1,0:T(8,128)(2,1)} collective-permute-done((bf16[324,512]{1,0:T(8,128)(2,1)S(1)}, bf16[324,512]{1,0:T(8,128)(2,1)}, u32[]{:S(2)}, u32[]{:S(2)}) %collective-permute-start.1) | collective-permute-done | bytes 331808 | tf_op jit(solution)/shard_map/ppermute | solution.py:118
  155.7 1.4 fusion.16
  157.3 0.8 pad.5
  158.1 13.2 %all-to-all-start = ((bf16[32,48,128]{2,1,0:T(8,128)(2,1)}), bf16[32,48,128]{2,1,0:T(8,128)(2,1)S(1)}, u32[]{:S(2)}, u32[]{:S(2)}) async-start(bf16[32,48,128]{2,1,0:T(8,128)(2,1)} %bitcast.15), calls=%async_computation.1 | async-start | bytes 786432 | tf_op jit(solution)/shard_map/all_to_all | solution.py:141
  171.5 13.9 %all-to-all-done = bf16[32,48,128]{2,1,0:T(8,128)(2,1)S(1)} async-done(((bf16[32,48,128]{2,1,0:T(8,128)(2,1)}), bf16[32,48,128]{2,1,0:T(8,128)(2,1)S(1)}, u32[]{:S(2)}, u32[]{:S(2)}) %all-to-all-start) | async-done | bytes 393248 | tf_op jit(solution)/shard_map/all_to_all | solution.py:141
  185.6 17.5 %all_to_all.10 = bf16[32,48,128]{2,1,0:T(8,128)(2,1)S(1)} all-to-all(bf16[32,48,128]{2,1,0:T(8,128)(2,1)S(1)} %fusion.17), channel_id=1, replica_groups=mesh['x'=4,'zl'=4,'c'=2,'y'=4,'zh'=2] {'x','zl','c'}, dimensions={0} | all-to-all | bytes 786432 | tf_op jit(solution)/shard_map/all_to_all | solution.py:143
  203.1 0.9 broadcast_in_dim_reshape_reshape.3
  (50 shorter events, 2.3 us)
Async XLA Ops:
  6.5 90.1 %copy-start = (bf16[256,4096]{1,0:T(8,128)(2,1)S(1)}, bf16[256,4096]{1,0:T(8,128)(2,1)}, u32[]{:S(2)}) copy-start(bf16[256,4096]{1,0:T(8,128)(2,1)} %param.17) | copy-start | bytes 6291460
  6.5 39.6 %all-gather.5.cloned.1.call-start = ((), (), s32[]{:S(2)}) async-start(), calls=%async_computation.4 | async-start | bytes 2621440 | tf_op jit(solution)/shard_map/all_gather | solution.py:175
  7.3 74.1 %all-gather.7.cloned.1.call-start = ((), (), s32[]{:S(2)}) async-start(), calls=%async_computation.5 | async-start | bytes 2621440 | tf_op jit(solution)/shard_map/all_gather | solution.py:176
  7.3 21.3 %collective-permute-start = (bf16[64,4096]{1,0:T(8,128)(2,1)}, bf16[64,4096]{1,0:T(8,128)(2,1)S(1)}, u32[]{:S(2)}, u32[]{:S(2)}) collective-permute-start(bf16[64,4096]{1,0:T(8,128)(2,1)} %param.11), channel_id=1, source_target_pairs={{0,1},{1,0},{2,3},{3,2},{4,5},{5,4},{6,7},{7,6},{8,9},{9,8},{10,11... | collective-permute-start | bytes 1572872 | tf_op jit(solution)/shard_map/ppermute | solution.py:118
  28.6 0.8 copy-start.4
  29.4 107.3 %reduce-scatter.2.cloned.1.call-start = ((), (), s32[]{:S(2)}) async-start(), calls=%async_computation.3 | async-start | bytes 3358720 | tf_op jit(solution)/shard_map/reduce_scatter | solution.py:229
  85.7 1.9 copy-start.1
  85.7 1.9 copy-start.5
  85.7 1.9 copy-start.6
  87.6 1.6 copy-start.8
  89.2 1.6 copy-start.9
  90.8 1.6 copy-start.10
  140.0 0.9 copy-start.2
  141.0 14.7 %collective-permute-start.1 = (bf16[324,512]{1,0:T(8,128)(2,1)S(1)}, bf16[324,512]{1,0:T(8,128)(2,1)}, u32[]{:S(2)}, u32[]{:S(2)}) collective-permute-start(bf16[324,512]{1,0:T(8,128)(2,1)S(1)} %select_bitcast_fusion), channel_id=1, source_target_pairs={{0,1},{1,0},{2,3},{3,2},{4,5},{5,4},{6,7},{7,6},{8,9},{9,8},{10,11... | collective-permute-start | bytes 995336 | tf_op jit(solution)/shard_map/ppermute | solution.py:118
  146.5 9.2 %copy-start.3 = (bf16[324,1,512]{2,1,0:T(2,128)(2,1)S(1)}, bf16[324,1,512]{2,1,0:T(2,128)(2,1)}, u32[]{:S(2)}) copy-start(bf16[324,1,512]{2,1,0:T(2,128)(2,1)} %copy-done.2) | copy-start | bytes 995332
  146.5 9.2 %copy-start.11 = (f32[512]{0:T(512)S(1)}, f32[512]{0:T(512)}, u32[]{:S(2)}) copy-start(f32[512]{0:T(512)} %param.18) | copy-start | bytes 6148
  148.5 22.8 %copy-start.7 = (s32[32,1]{0,1:T(1,128)S(1)}, s32[32,1]{0,1:T(1,128)}, u32[]{:S(2)}) copy-start(s32[32,1]{0,1:T(1,128)} %param.21) | copy-start | bytes 388
  158.1 27.3 %all-to-all-start = ((bf16[32,48,128]{2,1,0:T(8,128)(2,1)}), bf16[32,48,128]{2,1,0:T(8,128)(2,1)S(1)}, u32[]{:S(2)}, u32[]{:S(2)}) async-start(bf16[32,48,128]{2,1,0:T(8,128)(2,1)} %bitcast.15), calls=%async_computation.1 | async-start | bytes 786432 | tf_op jit(solution)/shard_map/all_to_all | solution.py:141
Sparse Core Ops, SparseCore 0:
  9.1 36.9 all-gather.4
  48.0 33.3 all-gather.6
  99.5 37.2 reduce-scatter.1
where the time goes:
time: 211 us; the launch traced here: 210 us
  waiting for transfers between devices  121 us (57%)
  starting transfers between devices  26.7 us (13%)
  blocking collectives  17.5 us (8%)
  between operations  14.9 us (7%)
  matrix products  10.8 us (5%)
  local copies, waits for them, and re-layouts  10.4 us (5%)
  other arithmetic  8.91 us (4%)
    reduce_scatter x1, waiting for transfers between devices, body(): lax.psum_scatter(partial_sum, 'y', scatter_dimension=1, tiled=True)  37.4 us
    all_gather x1, waiting for transfers between devices, body(): lax.all_gather(swap_pair(stream_rows), 'y', axis=0, tiled=False)  35.2 us
    ppermute x2, waiting for transfers between devices, swap_pair(): return lax.ppermute(array, 'zh', [(0, 1), (1, 0)])  20.6 us
    all_to_all x1, blocking collectives, shift_by_exchange(): back = lax.all_to_all(rolled, DP_AXES, 0, 0, tiled=True)  17.5 us
    all_to_all x1, waiting for transfers between devices, shift_by_exchange(): lax.all_to_all(flat.reshape(count, rows, lanes), DP_AXES, 0, 0, tiled=True)  13.9 us
    all_gather x1, waiting for transfers between devices, body(): own_blocks = lax.all_gather(stream_rows, 'y', axis=0, tiled=False)  13.5 us
    ppermute x2, starting transfers between devices, swap_pair(): return lax.ppermute(array, 'zh', [(0, 1), (1, 0)])  13.4 us
    all_to_all x1, starting transfers between devices, shift_by_exchange(): lax.all_to_all(flat.reshape(count, rows, lanes), DP_AXES, 0, 0, tiled=True)  13.2 us
  transfers between devices with their start and end apart: 6, of which 6 were waited for; matrix products, arithmetic and copies ran while one was open for 2% of the time, Pallas kernels for 0%

commit v1 on v0

--- a/solution.py
+++ b/solution.py
@@ -172,8 +172,20 @@
     feat_cols = scale_ls.shape[0]
 
     zh = lax.axis_index("zh")
+    y_index = lax.axis_index("y")
+    y_count = lax.axis_size("y")
     own_blocks = lax.all_gather(stream_rows, "y", axis=0, tiled=False)
-    partner_blocks = lax.all_gather(swap_pair(stream_rows), "y", axis=0, tiled=False)
+    partner = swap_pair(stream_rows)
+    live_blocks = -(-LIVE_ROWS // (2 * stream_rows.shape[0]))
+    candidates = [partner] + [
+        lax.ppermute(
+            partner, "y", [(src, (src + by) % y_count) for src in range(live_blocks)]
+        )
+        for by in range(1, y_count)
+    ]
+    slots = (y_index - jnp.arange(live_blocks, dtype=jnp.int32)) % y_count
+    partner_blocks = jnp.take(jnp.stack(candidates), slots, axis=0)
+    own_blocks = own_blocks[:live_blocks]
     live_rows = jnp.where(
         zh == 0,
         jnp.stack([own_blocks, partner_blocks], axis=1),

time: 211 us -> 205 us (0.972)
  waiting for transfers between devices: 121 us -> 98.3 us
  starting transfers between devices: 26.7 us -> 36.6 us
  local copies, waits for them, and re-layouts: 10.4 us -> 15.6 us
    all_gather x1 -> x0, waiting for transfers between devices: 35.2 us -> none  [body(): lax.all_gather(swap_pair(stream_rows), 'y', axis=0, tiled=False)]
    ppermute x0 -> x3, waiting for transfers between devices: none -> 29.6 us  [body(): lax.ppermute(partner, 'y', [(src, (src + by) % y_count) for src in range(...]
    all_gather x1, waiting for transfers between devices: 13.5 us -> 0.01 us  [body(): own_blocks = lax.all_gather(stream_rows, 'y', axis=0, tiled=False)]
    ppermute x0 -> x3, starting transfers between devices: none -> 10.1 us  [body(): lax.ppermute(partner, 'y', [(src, (src + by) % y_count) for src in range(...]
    select_n x1, other arithmetic: 4.28 us -> 0.46 us  [body(): jnp.where(zh == 0, jnp.stack([own_blocks, partner_blocks], axis=1), jnp.s...]
    gather x0 -> x1, local copies, waits for them, and re-layouts: none -> 3.48 us  [body(): partner_blocks = jnp.take(jnp.stack(candidates), slots, axis=0)]
    select_n x0 -> x2, other arithmetic: none -> 2.82 us  [body(): partner_blocks = jnp.take(jnp.stack(candidates), slots, axis=0)]
    ppermute x2, waiting for transfers between devices: 20.6 us -> 18.3 us  [swap_pair(): return lax.ppermute(array, 'zh', [(0, 1), (1, 0)])]
  transfers between devices with their start and end apart: 6 -> 8, of which waited for: 6 -> 6; matrix products, arithmetic and copies ran while one was open for 2% -> 6% of each run, Pallas kernels for 0% -> 0%
where the time goes in v1:
time: 205 us; the launch traced here: 204 us
  waiting for transfers between devices  98.3 us (48%)
  starting transfers between devices  36.6 us (18%)
  blocking collectives  17.5 us (9%)
  local copies, waits for them, and re-layouts  15.6 us (8%)
  between operations  15.2 us (7%)
  matrix products  11.5 us (6%)
  other arithmetic  9.5 us (5%)
    reduce_scatter x1, waiting for transfers between devices, body(): lax.psum_scatter(partial_sum, 'y', scatter_dimension=1, tiled=True)  36.4 us
    ppermute x3, waiting for transfers between devices, body(): lax.ppermute(partner, 'y', [(src, (src + by) % y_count) for src in range(...  29.6 us
    ppermute x2, waiting for transfers between devices, swap_pair(): return lax.ppermute(array, 'zh', [(0, 1), (1, 0)])  18.3 us
    all_to_all x1, blocking collectives, shift_by_exchange(): back = lax.all_to_all(rolled, DP_AXES, 0, 0, tiled=True)  17.5 us
    all_to_all x1, waiting for transfers between devices, shift_by_exchange(): lax.all_to_all(flat.reshape(count, rows, lanes), DP_AXES, 0, 0, tiled=True)  13.9 us
    ppermute x2, starting transfers between devices, swap_pair(): return lax.ppermute(array, 'zh', [(0, 1), (1, 0)])  13.3 us
    all_to_all x1, starting transfers between devices, shift_by_exchange(): lax.all_to_all(flat.reshape(count, rows, lanes), DP_AXES, 0, 0, tiled=True)  13.2 us
    ppermute x3, starting transfers between devices, body(): lax.ppermute(partner, 'y', [(src, (src + by) % y_count) for src in range(...  10.1 us
  transfers between devices with their start and end apart: 8, of which 6 were waited for; matrix products, arithmetic and copies ran while one was open for 6% of the time, Pallas kernels for 0%

profile of v1, /device:TPU:1, one launch (start us, length us, event | category | flops | bytes accessed | tf_op | source)
XLA Modules:
  0.0 204.1 jit_solution(6074211199644850611)
XLA Ops:
  6.5 7.7 %collective-permute-start = (bf16[64,4096]{1,0:T(8,128)(2,1)}, bf16[64,4096]{1,0:T(8,128)(2,1)S(1)}, u32[]{:S(2)}, u32[]{:S(2)}) collective-permute-start(bf16[64,4096]{1,0:T(8,128)(2,1)} %param.11), channel_id=1, source_target_pairs={{0,1},{1,0},{2,3},{3,2},{4,5},{5,4},{6,7},{7,6},{8,9},{9,8},{10,11... | collective-permute-start | bytes 1572872 | tf_op jit(solution)/shard_map/ppermute | solution.py:118
  16.6 11.2 %collective-permute-done = bf16[64,4096]{1,0:T(8,128)(2,1)S(1)} collective-permute-done((bf16[64,4096]{1,0:T(8,128)(2,1)}, bf16[64,4096]{1,0:T(8,128)(2,1)S(1)}, u32[]{:S(2)}, u32[]{:S(2)}) %collective-permute-start) | collective-permute-done | bytes 524320 | tf_op jit(solution)/shard_map/ppermute | solution.py:118
  27.7 3.7 %collective-permute-start.1 = (bf16[64,4096]{1,0:T(8,128)(2,1)S(1)}, bf16[64,4096]{1,0:T(8,128)(2,1)S(1)}, u32[]{:S(2)}, u32[]{:S(2)}) collective-permute-start(bf16[64,4096]{1,0:T(8,128)(2,1)S(1)} %collective-permute-done), channel_id=1, source_target_pairs={{0,2},{2,4},{4,6},{1,3},{3,5},{5,7},{8,10},{10,12},{12,14},{9,11},... | collective-permute-start | bytes 1572872 | tf_op jit(solution)/shard_map/ppermute | solution.py:181
  31.4 4.5 %collective-permute-start.2 = (bf16[64,4096]{1,0:T(8,128)(2,1)S(1)}, bf16[64,4096]{1,0:T(8,128)(2,1)S(1)}, u32[]{:S(2)}, u32[]{:S(2)}) collective-permute-start(bf16[64,4096]{1,0:T(8,128)(2,1)S(1)} %collective-permute-done), channel_id=1, source_target_pairs={{0,4},{2,6},{4,0},{1,5},{3,7},{5,1},{8,12},{10,14},{12,8},{9,13},{... | collective-permute-start | bytes 1572872 | tf_op jit(solution)/shard_map/ppermute | solution.py:181
  35.9 1.9 collective-permute-start.3
  38.8 14.2 %collective-permute-done.1 = bf16[64,4096]{1,0:T(8,128)(2,1)S(1)} collective-permute-done((bf16[64,4096]{1,0:T(8,128)(2,1)S(1)}, bf16[64,4096]{1,0:T(8,128)(2,1)S(1)}, u32[]{:S(2)}, u32[]{:S(2)}) %collective-permute-start.1) | collective-permute-done | bytes 524320 | tf_op jit(solution)/shard_map/ppermute | solution.py:181
  53.0 15.4 %collective-permute-done.2 = bf16[64,4096]{1,0:T(8,128)(2,1)S(1)} collective-permute-done((bf16[64,4096]{1,0:T(8,128)(2,1)S(1)}, bf16[64,4096]{1,0:T(8,128)(2,1)S(1)}, u32[]{:S(2)}, u32[]{:S(2)}) %collective-permute-start.2) | collective-permute-done | bytes 524320 | tf_op jit(solution)/shard_map/ppermute | solution.py:181
  68.4 1.6 pad_maximum_fusion
  70.0 3.5 %gather_fusion = bf16[3,64,4096]{2,1,0:T(8,128)(2,1)} fusion(bf16[4,64,4096]{2,1,0:T(8,128)(2,1)} %pad_maximum_fusion, s32[1024]{0:T(1024)S(1)} %pad_clamp_fusion), kind=kCustom, calls=%fused_computation | custom fusion | bytes 3145740 | tf_op jit(solution)/shard_map/jit(_take)/gather | solution.py:187
  73.4 2.8 %bitcast_select_fusion = bf16[3,1,64,4096]{3,2,1,0:T(8,128)(2,1)} fusion(bf16[3,64,4096]{2,1,0:T(8,128)(2,1)} %gather_fusion, pred[3]{0:T(512)(128)(4,1)S(1)} %compare_and_fusion), kind=kLoop, calls=%fused_computation.13 | loop fusion | flops 786432 | bytes 3145731 | tf_op jit(solution)/shard_map/jit(_take)/select_n | solution.py:187
  76.2 1.9 slice-done
  79.1 0.9 fusion.3
  80.3 1.4 fusion.6
  81.8 1.3 fusion.63
  83.4 1.3 fusion.62
  85.0 0.9 fusion.10
  86.1 1.5 fusion.61
  87.7 1.6 fusion.11
  89.3 2.7 %convolution_convert_fusion = bf16[328,4096]{1,0:T(8,128)(2,1)} fusion(bf16[256,4096]{1,0:T(8,128)(2,1)S(1)} %copy-done, s32[328]{0:T(512)S(1)} %concatenate.7, bf16[2,42,8,128]{3,2,1,0:T(8,128)(2,1)S(1)} %fusion.11), kind=kOutput, calls=%fused_computation.10 | convolution fusion | flops 745830016 | bytes 4957472 | tf_op jit(solution)/shard_map/dot_general | solution.py:226
  92.0 36.4 %reduce-scatter.2.cloned.1.call-done = bf16[328,1024]{1,0:T(8,128)(2,1)} async-done(((bf16[328,4096]{1,0:T(8,128)(2,1)}), bf16[328,1024]{1,0:T(8,128)(2,1)}) %reduce-scatter.2.cloned.1.call-update) | async-done | bytes 671760 | tf_op jit(solution)/shard_map/reduce_scatter | solution.py:241
  128.5 2.3 %slice.46 = bf16[324,2,512]{2,1,0:T(2,128)(2,1)S(1)} reshape(bf16[324,1024]{1,0:T(8,128)(2,1)} %bitcast.77) | data formatting | bytes 1327104 | tf_op jit(solution)/shard_map/slice | solution.py:242
  130.8 0.9 fusion.60
  131.7 0.8 copy-done.3
  132.7 5.5 %collective-permute-start.4 = (bf16[324,512]{1,0:T(8,128)(2,1)S(1)}, bf16[324,512]{1,0:T(8,128)(2,1)}, u32[]{:S(2)}, u32[]{:S(2)}) collective-permute-start(bf16[324,512]{1,0:T(8,128)(2,1)S(1)} %select_bitcast_fusion), channel_id=1, source_target_pairs={{0,1},{1,0},{2,3},{3,2},{4,5},{5,4},{6,7},{7,6},{8,9},{9,8},{10,11... | collective-permute-start | bytes 995336 | tf_op jit(solution)/shard_map/ppermute | solution.py:118
  138.2 2.0 slice.55
  140.2 7.2 %collective-permute-done.4 = bf16[324,512]{1,0:T(8,128)(2,1)} collective-permute-done((bf16[324,512]{1,0:T(8,128)(2,1)S(1)}, bf16[324,512]{1,0:T(8,128)(2,1)}, u32[]{:S(2)}, u32[]{:S(2)}) %collective-permute-start.4) | collective-permute-done | bytes 331808 | tf_op jit(solution)/shard_map/ppermute | solution.py:118
  147.4 2.1 %fusion.16 = bf16[324,512]{1,0:T(8,128)(2,1)} fusion(bf16[324,512]{1,0:T(8,128)(2,1)} %collective-permute-done.4, bf16[336,4096]{1,0:T(8,128)(2,1)S(1)} %slice.55, s32[]{:T(128)S(6)} %select_n.233, f32[512]{0:T(512)S(1)} %copy-done.11, pred[324]{0:T(512)(128)(4,1)S(1)} %broadcast_in_dim.66, pred[]{:T(512)S(6)} %eq.86, s32[324]{0:T(512)S(1)} %broadcast_select_fusion, ...), kind=kOutput, calls=%fused_computation.33 | convolution fusion | flops 112912704 | bytes 2339333 | tf_op jit(solution)/shard_map/dot_general | solution.py:235
  149.5 1.2 reshape.499
  151.5 13.2 %all-to-all-start = ((bf16[32,48,128]{2,1,0:T(8,128)(2,1)}), bf16[32,48,128]{2,1,0:T(8,128)(2,1)S(1)}, u32[]{:S(2)}, u32[]{:S(2)}) async-start(bf16[32,48,128]{2,1,0:T(8,128)(2,1)} %bitcast.20), calls=%async_computation.1 | async-start | bytes 786432 | tf_op jit(solution)/shard_map/all_to_all | solution.py:141
  164.8 13.9 %all-to-all-done = bf16[32,48,128]{2,1,0:T(8,128)(2,1)S(1)} async-done(((bf16[32,48,128]{2,1,0:T(8,128)(2,1)}), bf16[32,48,128]{2,1,0:T(8,128)(2,1)S(1)}, u32[]{:S(2)}, u32[]{:S(2)}) %all-to-all-start) | async-done | bytes 393248 | tf_op jit(solution)/shard_map/all_to_all | solution.py:141
  179.0 17.5 %all_to_all.10 = bf16[32,48,128]{2,1,0:T(8,128)(2,1)S(1)} all-to-all(bf16[32,48,128]{2,1,0:T(8,128)(2,1)S(1)} %fusion.17), channel_id=1, replica_groups=mesh['x'=4,'zl'=4,'c'=2,'y'=4,'zh'=2] {'x','zl','c'}, dimensions={0} | all-to-all | bytes 786432 | tf_op jit(solution)/shard_map/all_to_all | solution.py:143
  196.4 0.9 broadcast_in_dim_reshape_reshape.3
  (61 shorter events, 5.1 us)
Async XLA Ops:
  6.5 82.7 %copy-start = (bf16[256,4096]{1,0:T(8,128)(2,1)S(1)}, bf16[256,4096]{1,0:T(8,128)(2,1)}, u32[]{:S(2)}) copy-start(bf16[256,4096]{1,0:T(8,128)(2,1)} %param.17) | copy-start | bytes 6291460
  6.5 69.7 %all-gather.3.cloned.1.call-start = ((), (), s32[]{:S(2)}) async-start(), calls=%async_computation.4 | async-start | bytes 2621440 | tf_op jit(solution)/shard_map/all_gather | solution.py:177
  6.5 21.2 %collective-permute-start = (bf16[64,4096]{1,0:T(8,128)(2,1)}, bf16[64,4096]{1,0:T(8,128)(2,1)S(1)}, u32[]{:S(2)}, u32[]{:S(2)}) collective-permute-start(bf16[64,4096]{1,0:T(8,128)(2,1)} %param.11), channel_id=1, source_target_pairs={{0,1},{1,0},{2,3},{3,2},{4,5},{5,4},{6,7},{7,6},{8,9},{9,8},{10,11... | collective-permute-start | bytes 1572872 | tf_op jit(solution)/shard_map/ppermute | solution.py:118
  14.3 114.2 %reduce-scatter.2.cloned.1.call-start = ((), (), s32[]{:S(2)}) async-start(), calls=%async_computation.3 | async-start | bytes 3358720 | tf_op jit(solution)/shard_map/reduce_scatter | solution.py:241
  27.7 25.2 %collective-permute-start.1 = (bf16[64,4096]{1,0:T(8,128)(2,1)S(1)}, bf16[64,4096]{1,0:T(8,128)(2,1)S(1)}, u32[]{:S(2)}, u32[]{:S(2)}) collective-permute-start(bf16[64,4096]{1,0:T(8,128)(2,1)S(1)} %collective-permute-done), channel_id=1, source_target_pairs={{0,2},{2,4},{4,6},{1,3},{3,5},{5,7},{8,10},{10,12},{12,14},{9,11},... | collective-permute-start | bytes 1572872 | tf_op jit(solution)/shard_map/ppermute | solution.py:181
  31.4 37.0 %collective-permute-start.2 = (bf16[64,4096]{1,0:T(8,128)(2,1)S(1)}, bf16[64,4096]{1,0:T(8,128)(2,1)S(1)}, u32[]{:S(2)}, u32[]{:S(2)}) collective-permute-start(bf16[64,4096]{1,0:T(8,128)(2,1)S(1)} %collective-permute-done), channel_id=1, source_target_pairs={{0,4},{2,6},{4,0},{1,5},{3,7},{5,1},{8,12},{10,14},{12,8},{9,13},{... | collective-permute-start | bytes 1572872 | tf_op jit(solution)/shard_map/ppermute | solution.py:181
  35.9 32.5 %collective-permute-start.3 = (bf16[64,4096]{1,0:T(8,128)(2,1)S(1)}, bf16[64,4096]{1,0:T(8,128)(2,1)S(1)}, u32[]{:S(2)}, u32[]{:S(2)}) collective-permute-start(bf16[64,4096]{1,0:T(8,128)(2,1)S(1)} %collective-permute-done), channel_id=1, source_target_pairs={{0,6},{2,0},{4,2},{1,7},{3,1},{5,3},{8,14},{10,8},{12,10},{9,15},{... | collective-permute-start | bytes 1572872 | tf_op jit(solution)/shard_map/ppermute | solution.py:181
  76.2 1.9 slice-start
  76.2 1.9 copy-start.2
  78.6 1.6 copy-start.1
  78.6 1.6 copy-start.5
  78.6 1.6 copy-start.6
  80.3 1.6 copy-start.8
  81.8 1.6 copy-start.9
  83.4 1.6 copy-start.10
  131.7 0.9 copy-start.3
  132.7 14.7 %collective-permute-start.4 = (bf16[324,512]{1,0:T(8,128)(2,1)S(1)}, bf16[324,512]{1,0:T(8,128)(2,1)}, u32[]{:S(2)}, u32[]{:S(2)}) collective-permute-start(bf16[324,512]{1,0:T(8,128)(2,1)S(1)} %select_bitcast_fusion), channel_id=1, source_target_pairs={{0,1},{1,0},{2,3},{3,2},{4,5},{5,4},{6,7},{7,6},{8,9},{9,8},{10,11... | collective-permute-start | bytes 995336 | tf_op jit(solution)/shard_map/ppermute | solution.py:118
  138.2 9.2 %copy-start.4 = (bf16[324,1,512]{2,1,0:T(2,128)(2,1)S(1)}, bf16[324,1,512]{2,1,0:T(2,128)(2,1)}, u32[]{:S(2)}) copy-start(bf16[324,1,512]{2,1,0:T(2,128)(2,1)} %copy-done.3) | copy-start | bytes 995332
  138.2 9.2 %copy-start.11 = (f32[512]{0:T(512)S(1)}, f32[512]{0:T(512)}, u32[]{:S(2)}) copy-start(f32[512]{0:T(512)} %param.18) | copy-start | bytes 6148
  140.2 24.5 %copy-start.7 = (s32[32,1]{0,1:T(1,128)S(1)}, s32[32,1]{0,1:T(1,128)}, u32[]{:S(2)}) copy-start(s32[32,1]{0,1:T(1,128)} %param.21) | copy-start | bytes 388
  151.5 27.2 %all-to-all-start = ((bf16[32,48,128]{2,1,0:T(8,128)(2,1)}), bf16[32,48,128]{2,1,0:T(8,128)(2,1)S(1)}, u32[]{:S(2)}, u32[]{:S(2)}) async-start(bf16[32,48,128]{2,1,0:T(8,128)(2,1)} %bitcast.20), calls=%async_computation.1 | async-start | bytes 786432 | tf_op jit(solution)/shard_map/all_to_all | solution.py:141
Sparse Core Ops, SparseCore 0:
  14.4 44.4 all-gather.2
  92.1 36.2 reduce-scatter.1

commit v2 on v1

--- a/solution.py
+++ b/solution.py
@@ -28,8 +28,7 @@
     )
 
 
-def row_layout(side_row, offset_row, count):
-    row_ids = jnp.arange(count, dtype=jnp.int32)
+def row_layout(side_row, offset_row, row_ids):
     lengths = EXTRA + side_row * side_row
     inside = (
         (row_ids[:, None] >= offset_row[None, :])
@@ -110,6 +109,11 @@
     ).astype(jnp.bfloat16)
 
 
+def position_of(rows, row_ids):
+    hits = rows[:, None] == row_ids[None, :]
+    return jnp.argmax(hits, axis=1).astype(jnp.int32)
+
+
 def one_hot(rows, count):
     return (rows[:, None] == jnp.arange(count, dtype=jnp.int32)[None, :]).astype(jnp.bfloat16)
 
@@ -183,14 +187,16 @@
         )
         for by in range(1, y_count)
     ]
-    slots = (y_index - jnp.arange(live_blocks, dtype=jnp.int32)) % y_count
-    partner_blocks = jnp.take(jnp.stack(candidates), slots, axis=0)
-    own_blocks = own_blocks[:live_blocks]
-    live_rows = jnp.where(
-        zh == 0,
-        jnp.stack([own_blocks, partner_blocks], axis=1),
-        jnp.stack([partner_blocks, own_blocks], axis=1),
-    ).reshape(-1, stream_rows.shape[1])[:LIVE_ROWS]
+    block = stream_rows.shape[0]
+    in_block = jnp.arange(block, dtype=jnp.int32)
+    own_ids = (2 * jnp.arange(live_blocks, dtype=jnp.int32)[:, None] + zh) * block + in_block
+    from_y = (y_index - jnp.arange(y_count, dtype=jnp.int32)) % y_count
+    partner_ids = (2 * from_y[:, None] + 1 - zh) * block + in_block
+    row_ids = jnp.concatenate([own_ids.reshape(-1), partner_ids.reshape(-1)])
+    live_rows = jnp.concatenate(
+        [own_blocks[:live_blocks].reshape(-1, stream_rows.shape[1])] + candidates, axis=0
+    )
+    row_count = row_ids.shape[0]
     normed = layer_norm(live_rows, ln_gain, ln_bias)
 
     projected = jnp.concatenate(
@@ -201,27 +207,27 @@
         ],
         axis=1,
     )
-    segment, coord_one, coord_two = row_layout(side_row, offset_row, LIVE_ROWS)
+    segment, coord_one, coord_two = row_layout(side_row, offset_row, row_ids)
     cosine, sine_tab = rotary_tables(coord_one, coord_two, HEAD)
     queries = rotate(
-        projected[:, :head_cols].reshape(LIVE_ROWS, local_heads, HEAD), cosine, sine_tab
+        projected[:, :head_cols].reshape(row_count, local_heads, HEAD), cosine, sine_tab
     ).astype(jnp.bfloat16)
     key_rows = rotate(
-        projected[:, head_cols : 2 * head_cols].reshape(LIVE_ROWS, local_heads, HEAD),
+        projected[:, head_cols : 2 * head_cols].reshape(row_count, local_heads, HEAD),
         cosine,
         sine_tab,
     ).astype(jnp.bfloat16)
     value_rows = (
-        projected[:, 2 * head_cols :].astype(jnp.bfloat16).reshape(LIVE_ROWS, local_heads, HEAD)
-    )
-    attended = attention(queries, key_rows, value_rows, segment).reshape(LIVE_ROWS, head_cols)
+        projected[:, 2 * head_cols :].astype(jnp.bfloat16).reshape(row_count, local_heads, HEAD)
+    )
+    attended = attention(queries, key_rows, value_rows, segment).reshape(row_count, head_cols)
 
     source_rows, valid = merge_rows(side_row[0], offset_row[0])
     padded_rows = jnp.concatenate(
         [source_rows, jnp.zeros((MERGE_PAD - source_rows.shape[0],), jnp.int32)]
     )
     merged_attended = jnp.dot(
-        one_hot(padded_rows, LIVE_ROWS), attended, preferred_element_type=jnp.float32
+        one_hot(position_of(padded_rows, row_ids), row_count), attended, preferred_element_type=jnp.float32
     ).astype(jnp.bfloat16)
     partial_sum = jnp.dot(merged_attended, w_o, preferred_element_type=jnp.float32).astype(
         jnp.bfloat16
@@ -233,7 +239,7 @@
 
     feat_index = lax.axis_index("y") * lax.axis_size("zh") + zh
     residual = jnp.dot(
-        one_hot(source_rows, LIVE_ROWS),
+        one_hot(position_of(source_rows, row_ids), row_count),
         lax.dynamic_slice_in_dim(live_rows, feat_index * feat_cols, feat_cols, axis=1),
         preferred_element_type=jnp.float32,
     )

time: 205 us -> 202 us (0.985)
  local copies, waits for them, and re-layouts: 15.6 us -> 11.7 us
    ppermute x3, waiting for transfers between devices: 29.6 us -> 7.25 us  [body(): lax.ppermute(partner, 'y', [(src, (src + by) % y_count) for src in range(...]
    all_gather x1, waiting for transfers between devices: 0.01 us -> 16.9 us  [body(): own_blocks = lax.all_gather(stream_rows, 'y', axis=0, tiled=False)]
    reduce_scatter x1, waiting for transfers between devices: 36.4 us -> 42.6 us  [body(): lax.psum_scatter(partial_sum, 'y', scatter_dimension=1, tiled=True)]
    slice x3 -> x0, local copies, waits for them, and re-layouts: 3.9 us -> none  [the longest x1 2.02 us: body(): jnp.where(zh == 0, jnp.stack([own_blocks, partner_blocks], axis=1), jnp.s...]
    gather x1 -> x0, local copies, waits for them, and re-layouts: 3.48 us -> none  [body(): partner_blocks = jnp.take(jnp.stack(candidates), slots, axis=0)]
    select_n x4 -> x1, other arithmetic: 3.42 us -> 0.21 us  [row_layout(): jnp.where(is_patch, (2 * across + 1).astype(jnp.float32) / side_float - 1...]
    unnamed x24, local copies, waits for them, and re-layouts: 1.77 us -> 4.9 us
  transfers between devices with their start and end apart: 8 -> 8, of which waited for: 6 -> 6; matrix products, arithmetic and copies ran while one was open for 6% -> 4% of each run, Pallas kernels for 0% -> 0%
where the time goes in v2:
time: 202 us; the launch traced here: 201 us
  waiting for transfers between devices  98.4 us (49%)
  starting transfers between devices  37.1 us (18%)
  blocking collectives  17.5 us (9%)
  between operations  15.2 us (8%)
  matrix products  13.2 us (7%)
  local copies, waits for them, and re-layouts  11.7 us (6%)
  other arithmetic  8.18 us (4%)
    reduce_scatter x1, waiting for transfers between devices, body(): lax.psum_scatter(partial_sum, 'y', scatter_dimension=1, tiled=True)  42.6 us
    all_to_all x1, blocking collectives, shift_by_exchange(): back = lax.all_to_all(rolled, DP_AXES, 0, 0, tiled=True)  17.5 us
    ppermute x2, waiting for transfers between devices, swap_pair(): return lax.ppermute(array, 'zh', [(0, 1), (1, 0)])  17.1 us
    all_gather x1, waiting for transfers between devices, body(): own_blocks = lax.all_gather(stream_rows, 'y', axis=0, tiled=False)  16.9 us
    all_to_all x1, waiting for transfers between devices, shift_by_exchange(): lax.all_to_all(flat.reshape(count, rows, lanes), DP_AXES, 0, 0, tiled=True)  13.9 us
    ppermute x2, starting transfers between devices, swap_pair(): return lax.ppermute(array, 'zh', [(0, 1), (1, 0)])  13.4 us
    all_to_all x1, starting transfers between devices, shift_by_exchange(): lax.all_to_all(flat.reshape(count, rows, lanes), DP_AXES, 0, 0, tiled=True)  13.2 us
    ppermute x3, starting transfers between devices, body(): lax.ppermute(partner, 'y', [(src, (src + by) % y_count) for src in range(...  10.5 us
  transfers between devices with their start and end apart: 8, of which 6 were waited for; matrix products, arithmetic and copies ran while one was open for 4% of the time, Pallas kernels for 0%

profile of v2, /device:TPU:1, one launch (start us, length us, event | category | flops | bytes accessed | tf_op | source)
XLA Modules:
  0.0 201.2 jit_solution(16235335787025157621)
XLA Ops:
  7.3 7.8 %collective-permute-start = (bf16[64,4096]{1,0:T(8,128)(2,1)}, bf16[64,4096]{1,0:T(8,128)(2,1)S(1)}, u32[]{:S(2)}, u32[]{:S(2)}) collective-permute-start(bf16[64,4096]{1,0:T(8,128)(2,1)} %param.11), channel_id=1, source_target_pairs={{0,1},{1,0},{2,3},{3,2},{4,5},{5,4},{6,7},{7,6},{8,9},{9,8},{10,11... | collective-permute-start | bytes 1572872 | tf_op jit(solution)/shard_map/ppermute | solution.py:122
  18.0 1.0 fusion.26
  19.0 0.9 iota_reduce_fusion
  19.9 8.7 %collective-permute-done = bf16[64,4096]{1,0:T(8,128)(2,1)S(1)} collective-permute-done((bf16[64,4096]{1,0:T(8,128)(2,1)}, bf16[64,4096]{1,0:T(8,128)(2,1)S(1)}, u32[]{:S(2)}, u32[]{:S(2)}) %collective-permute-start) | collective-permute-done | bytes 524320 | tf_op jit(solution)/shard_map/ppermute | solution.py:122
  28.6 5.1 %collective-permute-start.3 = (bf16[64,4096]{1,0:T(8,128)(2,1)S(1)}, bf16[64,4096]{1,0:T(8,128)(2,1)}, u32[]{:S(2)}, u32[]{:S(2)}) collective-permute-start(bf16[64,4096]{1,0:T(8,128)(2,1)S(1)} %collective-permute-done), channel_id=1, source_target_pairs={{0,6},{2,0},{4,2},{1,7},{3,1},{5,3},{8,14},{10,8},{12,10},{9,15},{... | collective-permute-start | bytes 1572872 | tf_op jit(solution)/shard_map/ppermute | solution.py:185
  33.7 3.0 %collective-permute-start.2 = (bf16[64,4096]{1,0:T(8,128)(2,1)S(1)}, bf16[64,4096]{1,0:T(8,128)(2,1)}, u32[]{:S(2)}, u32[]{:S(2)}) collective-permute-start(bf16[64,4096]{1,0:T(8,128)(2,1)S(1)} %collective-permute-done), channel_id=1, source_target_pairs={{0,4},{2,6},{4,0},{1,5},{3,7},{5,1},{8,12},{10,14},{12,8},{9,13},{... | collective-permute-start | bytes 1572872 | tf_op jit(solution)/shard_map/ppermute | solution.py:185
  36.7 2.3 %collective-permute-start.1 = (bf16[64,4096]{1,0:T(8,128)(2,1)S(1)}, bf16[64,4096]{1,0:T(8,128)(2,1)}, u32[]{:S(2)}, u32[]{:S(2)}) collective-permute-start(bf16[64,4096]{1,0:T(8,128)(2,1)S(1)} %collective-permute-done), channel_id=1, source_target_pairs={{0,2},{2,4},{4,6},{1,3},{3,5},{5,7},{8,10},{10,12},{12,14},{9,11},... | collective-permute-start | bytes 1572872 | tf_op jit(solution)/shard_map/ppermute | solution.py:185
  39.1 16.9 %all-gather.3.cloned.1.call-done = bf16[256,4096]{1,0:T(8,128)(2,1)} async-done(((bf16[64,4096]{1,0:T(8,128)(2,1)}), bf16[256,4096]{1,0:T(8,128)(2,1)}) %all-gather.3.cloned.1.call-update) | async-done | bytes 2097168 | tf_op jit(solution)/shard_map/all_gather | solution.py:181
  55.9 1.5 slice_dynamic-update-slice_fusion
  57.5 7.2 %collective-permute-done.1 = bf16[64,4096]{1,0:T(8,128)(2,1)} collective-permute-done((bf16[64,4096]{1,0:T(8,128)(2,1)S(1)}, bf16[64,4096]{1,0:T(8,128)(2,1)}, u32[]{:S(2)}, u32[]{:S(2)}) %collective-permute-start.1) | collective-permute-done | bytes 524320 | tf_op jit(solution)/shard_map/ppermute | solution.py:185
  64.7 1.1 constant_dynamic-update-slice_fusion.2
  65.8 1.1 constant_dynamic-update-slice_fusion.1
  66.9 1.1 constant_dynamic-update-slice_fusion
  68.6 1.1 fusion.3
  69.8 2.1 %fusion.6 = bf16[448,4096]{1,0:T(8,128)(2,1)S(1)} fusion(bf16[448,4096]{1,0:T(8,128)(2,1)S(1)} %constant_dynamic-update-slice_fusion, f32[4096]{0:T(1024)S(1)} %copy-done.3, f32[4096]{0:T(1024)S(1)} %copy-done.4, f32[448]{0:T(512)S(1)} %add_rsqrt_fusion, f32[448]{0:T(512)S(1)} %broadcast_multiply_fusion), kind=kLoop, calls=%fused_computation.8 | loop fusion | flops 11010048 | bytes 7376384 | tf_op jit(solution)/shard_map/convert_element_type | solution.py:26
  71.9 1.8 fusion.11
  73.8 1.3 fusion.62
  75.3 1.3 fusion.61
  77.2 2.2 %fusion.60 = (f32[2,448]{1,0:T(2,128)S(1)}, f32[2,448,448]{1,2,0:T(8,128)}) fusion(pred[448,448]{0,1:T(8,128)(4,1)S(1)} %broadcast_compare_fusion, bf16[448,2,128]{0,2,1:T(8,128)(2,1)S(1)} %get-tuple-element.12, bf16[448,2,128]{0,2,1:T(8,128)(2,1)S(1)} %get-tuple-element.11), kind=kOutput, calls=%fused_computation.120 | convolution fusion | flops 104366528 | bytes 2268672 | tf_op jit(solution)/shard_map/sub | solution.py:78
  79.3 2.1 %fusion.10 = bf16[2,56,8,128]{3,2,1,0:T(8,128)(2,1)S(1)} fusion(f32[2,448,448]{1,2,0:T(8,128)} %get-tuple-element.24, f32[2,448]{1,0:T(2,128)S(1)} %get-tuple-element.23, bf16[56,2,8,128]{3,2,1,0:T(8,128)(2,1)} %fusion.11), kind=kOutput, calls=%fused_computation.21 | convolution fusion | flops 103677952 | bytes 2067968 | tf_op jit(solution)/shard_map/hqk,khd->qhd/dot_general | solution.py:107
  81.5 2.7 %convolution_convert_fusion = bf16[328,4096]{1,0:T(8,128)(2,1)} fusion(bf16[256,4096]{1,0:T(8,128)(2,1)S(1)} %copy-done, s32[328]{0:T(512)S(1)} %get-tuple-element.8, bf16[2,56,8,128]{3,2,1,0:T(8,128)(2,1)S(1)} %fusion.10), kind=kOutput, calls=%fused_computation.9 | convolution fusion | flops 764675584 | bytes 5014816 | tf_op jit(solution)/shard_map/dot_general | solution.py:232
  84.2 42.6 %reduce-scatter.2.cloned.1.call-done = bf16[328,1024]{1,0:T(8,128)(2,1)} async-done(((bf16[328,4096]{1,0:T(8,128)(2,1)}), bf16[328,1024]{1,0:T(8,128)(2,1)}) %reduce-scatter.2.cloned.1.call-update) | async-done | bytes 671760 | tf_op jit(solution)/shard_map/reduce_scatter | solution.py:247
  126.8 2.3 %slice.42 = bf16[324,2,512]{2,1,0:T(2,128)(2,1)S(1)} reshape(bf16[324,1024]{1,0:T(8,128)(2,1)} %bitcast.62) | data formatting | bytes 1327104 | tf_op jit(solution)/shard_map/slice | solution.py:248
  129.2 0.9 fusion.59
  131.0 5.6 %collective-permute-start.4 = (bf16[324,512]{1,0:T(8,128)(2,1)S(1)}, bf16[324,512]{1,0:T(8,128)(2,1)}, u32[]{:S(2)}, u32[]{:S(2)}) collective-permute-start(bf16[324,512]{1,0:T(8,128)(2,1)S(1)} %select_bitcast_fusion), channel_id=1, source_target_pairs={{0,1},{1,0},{2,3},{3,2},{4,5},{5,4},{6,7},{7,6},{8,9},{9,8},{10,11... | collective-permute-start | bytes 995336 | tf_op jit(solution)/shard_map/ppermute | solution.py:122
  136.6 0.9 iota_reduce_fusion.1
  137.4 8.3 %collective-permute-done.4 = bf16[324,512]{1,0:T(8,128)(2,1)} collective-permute-done((bf16[324,512]{1,0:T(8,128)(2,1)S(1)}, bf16[324,512]{1,0:T(8,128)(2,1)}, u32[]{:S(2)}, u32[]{:S(2)}) %collective-permute-start.4) | collective-permute-done | bytes 331808 | tf_op jit(solution)/shard_map/ppermute | solution.py:122
  145.8 1.8 fusion.9
  148.5 13.2 %all-to-all-start = ((bf16[32,48,128]{2,1,0:T(8,128)(2,1)}), bf16[32,48,128]{2,1,0:T(8,128)(2,1)S(1)}, u32[]{:S(2)}, u32[]{:S(2)}) async-start(bf16[32,48,128]{2,1,0:T(8,128)(2,1)} %bitcast.12), calls=%async_computation.1 | async-start | bytes 786432 | tf_op jit(solution)/shard_map/all_to_all | solution.py:145
  161.9 13.9 %all-to-all-done = bf16[32,48,128]{2,1,0:T(8,128)(2,1)S(1)} async-done(((bf16[32,48,128]{2,1,0:T(8,128)(2,1)}), bf16[32,48,128]{2,1,0:T(8,128)(2,1)S(1)}, u32[]{:S(2)}, u32[]{:S(2)}) %all-to-all-start) | async-done | bytes 393248 | tf_op jit(solution)/shard_map/all_to_all | solution.py:145
  176.0 17.5 %all_to_all.10 = bf16[32,48,128]{2,1,0:T(8,128)(2,1)S(1)} all-to-all(bf16[32,48,128]{2,1,0:T(8,128)(2,1)S(1)} %fusion.21), channel_id=1, replica_groups=mesh['x'=4,'zl'=4,'c'=2,'y'=4,'zh'=2] {'x','zl','c'}, dimensions={0} | all-to-all | bytes 786432 | tf_op jit(solution)/shard_map/all_to_all | solution.py:147
  193.5 0.9 broadcast_in_dim_reshape_reshape.3
  (60 shorter events, 5.8 us)
Async XLA Ops:
  6.5 75.0 %copy-start = (bf16[256,4096]{1,0:T(8,128)(2,1)S(1)}, bf16[256,4096]{1,0:T(8,128)(2,1)}, u32[]{:S(2)}) copy-start(bf16[256,4096]{1,0:T(8,128)(2,1)} %param.17) | copy-start | bytes 6291460
  6.5 49.4 %all-gather.3.cloned.1.call-start = ((), (), s32[]{:S(2)}) async-start(), calls=%async_computation.4 | async-start | bytes 2621440 | tf_op jit(solution)/shard_map/all_gather | solution.py:181
  7.3 119.6 %reduce-scatter.2.cloned.1.call-start = ((), (), s32[]{:S(2)}) async-start(), calls=%async_computation.3 | async-start | bytes 3358720 | tf_op jit(solution)/shard_map/reduce_scatter | solution.py:247
  7.3 21.3 %collective-permute-start = (bf16[64,4096]{1,0:T(8,128)(2,1)}, bf16[64,4096]{1,0:T(8,128)(2,1)S(1)}, u32[]{:S(2)}, u32[]{:S(2)}) collective-permute-start(bf16[64,4096]{1,0:T(8,128)(2,1)} %param.11), channel_id=1, source_target_pairs={{0,1},{1,0},{2,3},{3,2},{4,5},{5,4},{6,7},{7,6},{8,9},{9,8},{10,11... | collective-permute-start | bytes 1572872 | tf_op jit(solution)/shard_map/ppermute | solution.py:122
  28.6 38.3 %collective-permute-start.3 = (bf16[64,4096]{1,0:T(8,128)(2,1)S(1)}, bf16[64,4096]{1,0:T(8,128)(2,1)}, u32[]{:S(2)}, u32[]{:S(2)}) collective-permute-start(bf16[64,4096]{1,0:T(8,128)(2,1)S(1)} %collective-permute-done), channel_id=1, source_target_pairs={{0,6},{2,0},{4,2},{1,7},{3,1},{5,3},{8,14},{10,8},{12,10},{9,15},{... | collective-permute-start | bytes 1572872 | tf_op jit(solution)/shard_map/ppermute | solution.py:185
  33.7 32.1 %collective-permute-start.2 = (bf16[64,4096]{1,0:T(8,128)(2,1)S(1)}, bf16[64,4096]{1,0:T(8,128)(2,1)}, u32[]{:S(2)}, u32[]{:S(2)}) collective-permute-start(bf16[64,4096]{1,0:T(8,128)(2,1)S(1)} %collective-permute-done), channel_id=1, source_target_pairs={{0,4},{2,6},{4,0},{1,5},{3,7},{5,1},{8,12},{10,14},{12,8},{9,13},{... | collective-permute-start | bytes 1572872 | tf_op jit(solution)/shard_map/ppermute | solution.py:185
  36.7 28.0 %collective-permute-start.1 = (bf16[64,4096]{1,0:T(8,128)(2,1)S(1)}, bf16[64,4096]{1,0:T(8,128)(2,1)}, u32[]{:S(2)}, u32[]{:S(2)}) collective-permute-start(bf16[64,4096]{1,0:T(8,128)(2,1)S(1)} %collective-permute-done), channel_id=1, source_target_pairs={{0,2},{2,4},{4,6},{1,3},{3,5},{5,7},{8,10},{10,12},{12,14},{9,11},... | collective-permute-start | bytes 1572872 | tf_op jit(solution)/shard_map/ppermute | solution.py:185
  68.0 1.8 copy-start.1
  68.0 1.8 copy-start.3
  68.0 1.8 copy-start.4
  69.8 2.1 %copy-start.6 = (bf16[4096,256]{1,0:T(8,128)(2,1)S(1)}, bf16[4096,256]{1,0:T(8,128)(2,1)}, u32[]{:S(2)}) copy-start(bf16[4096,256]{1,0:T(8,128)(2,1)} %param.16) | copy-start | bytes 6291460
  71.9 1.8 copy-start.7
  73.7 1.6 copy-start.8
  84.2 61.6 %copy-start.9 = (f32[512]{0:T(512)S(1)}, f32[512]{0:T(512)}, u32[]{:S(2)}) copy-start(f32[512]{0:T(512)} %param.18) | copy-start | bytes 6148
  130.1 0.8 copy-start.2
  130.1 31.6 %copy-start.5 = (s32[32,1]{0,1:T(1,128)S(1)}, s32[32,1]{0,1:T(1,128)}, u32[]{:S(2)}) copy-start(s32[32,1]{0,1:T(1,128)} %param.21) | copy-start | bytes 388
  131.0 14.7 %collective-permute-start.4 = (bf16[324,512]{1,0:T(8,128)(2,1)S(1)}, bf16[324,512]{1,0:T(8,128)(2,1)}, u32[]{:S(2)}, u32[]{:S(2)}) collective-permute-start(bf16[324,512]{1,0:T(8,128)(2,1)S(1)} %select_bitcast_fusion), channel_id=1, source_target_pairs={{0,1},{1,0},{2,3},{3,2},{4,5},{5,4},{6,7},{7,6},{8,9},{9,8},{10,11... | collective-permute-start | bytes 995336 | tf_op jit(solution)/shard_map/ppermute | solution.py:122
  148.5 27.3 %all-to-all-start = ((bf16[32,48,128]{2,1,0:T(8,128)(2,1)}), bf16[32,48,128]{2,1,0:T(8,128)(2,1)S(1)}, u32[]{:S(2)}, u32[]{:S(2)}) async-start(bf16[32,48,128]{2,1,0:T(8,128)(2,1)} %bitcast.12), calls=%async_computation.1 | async-start | bytes 786432 | tf_op jit(solution)/shard_map/all_to_all | solution.py:145
Sparse Core Ops, SparseCore 0:
  9.1 46.7 all-gather.2
  84.4 42.4 reduce-scatter.1

commit v3 on v2

--- a/solution.py
+++ b/solution.py
@@ -244,7 +244,19 @@
         preferred_element_type=jnp.float32,
     )
 
-    quarter = lax.psum_scatter(partial_sum, "y", scatter_dimension=1, tiled=True)
+    quarter_cols = feat_cols * lax.axis_size("zh")
+    on_sc = MERGE_PAD // 2
+    quarter_sc = lax.psum_scatter(partial_sum[:on_sc], "y", scatter_dimension=1, tiled=True)
+    rest = partial_sum[on_sc:]
+    quarter_pp = lax.dynamic_slice_in_dim(rest, y_index * quarter_cols, quarter_cols, axis=1)
+    quarter_pp = quarter_pp.astype(jnp.float32)
+    for by in range(1, y_count):
+        chunk = lax.dynamic_slice_in_dim(
+            rest, ((y_index + by) % y_count) * quarter_cols, quarter_cols, axis=1
+        )
+        moved = lax.ppermute(chunk, "y", [(src, (src + by) % y_count) for src in range(y_count)])
+        quarter_pp = quarter_pp + moved.astype(jnp.float32)
+    quarter = jnp.concatenate([quarter_sc, quarter_pp.astype(jnp.bfloat16)], axis=0)
     split = quarter.reshape(MERGE_PAD, 2, feat_cols)[: source_rows.shape[0]]
     mine = jnp.where(zh == 0, split[:, 0], split[:, 1])
     theirs = jnp.where(zh == 0, split[:, 1], split[:, 0])

time: 202 us -> 197 us (0.975)
  waiting for transfers between devices: 98.4 us -> 79.6 us
  starting transfers between devices: 37.1 us -> 45.1 us
  other arithmetic: 8.18 us -> 11.5 us
  local copies, waits for them, and re-layouts: 11.7 us -> 13.9 us
    reduce_scatter x1, waiting for transfers between devices: 42.6 us -> 10.6 us  [body(): lax.psum_scatter(partial_sum[:on_sc], 'y', scatter_dimension=1, tiled=True)]
    ppermute x0 -> x3, waiting for transfers between devices: none -> 14.6 us  [body(): lax.ppermute(chunk, 'y', [(src, (src + by) % y_count) for src in range(y_...]
    ppermute x0 -> x3, starting transfers between devices: none -> 5.73 us  [body(): lax.ppermute(chunk, 'y', [(src, (src + by) % y_count) for src in range(y_...]
    all_to_all x1, starting transfers between devices: 13.2 us -> 16.8 us  [shift_by_exchange(): lax.all_to_all(flat.reshape(count, rows, lanes), DP_AXES, 0, 0, tiled=True)]
    slice x0 -> x1, local copies, waits for them, and re-layouts: none -> 3.19 us  [body(): partial_sum[:on_sc]]
    convert_element_type x0 -> x1, other arithmetic: none -> 2.16 us  [body(): quarter_pp.astype(jnp.bfloat16)]
  transfers between devices with their start and end apart: 8 -> 11, of which waited for: 6 -> 8; matrix products, arithmetic and copies ran while one was open for 4% -> 6% of each run, Pallas kernels for 0% -> 0%
where the time goes in v3:
time: 197 us; the launch traced here: 196 us
  waiting for transfers between devices  79.6 us (40%)
  starting transfers between devices  45.1 us (23%)
  blocking collectives  17.5 us (9%)
  between operations  15.3 us (8%)
  local copies, waits for them, and re-layouts  13.9 us (7%)
  matrix products  13.1 us (7%)
  other arithmetic  11.5 us (6%)
    all_to_all x1, blocking collectives, shift_by_exchange(): back = lax.all_to_all(rolled, DP_AXES, 0, 0, tiled=True)  17.5 us
    all_gather x1, waiting for transfers between devices, body(): own_blocks = lax.all_gather(stream_rows, 'y', axis=0, tiled=False)  16.9 us
    all_to_all x1, starting transfers between devices, shift_by_exchange(): lax.all_to_all(flat.reshape(count, rows, lanes), DP_AXES, 0, 0, tiled=True)  16.8 us
    ppermute x2, waiting for transfers between devices, swap_pair(): return lax.ppermute(array, 'zh', [(0, 1), (1, 0)])  15.6 us
    ppermute x3, waiting for transfers between devices, body(): lax.ppermute(chunk, 'y', [(src, (src + by) % y_count) for src in range(y_...  14.6 us
    all_to_all x1, waiting for transfers between devices, shift_by_exchange(): lax.all_to_all(flat.reshape(count, rows, lanes), DP_AXES, 0, 0, tiled=True)  13.9 us
    ppermute x2, starting transfers between devices, swap_pair(): return lax.ppermute(array, 'zh', [(0, 1), (1, 0)])  12.1 us
    reduce_scatter x1, waiting for transfers between devices, body(): lax.psum_scatter(partial_sum[:on_sc], 'y', scatter_dimension=1, tiled=True)  10.6 us
  transfers between devices with their start and end apart: 11, of which 8 were waited for; matrix products, arithmetic and copies ran while one was open for 6% of the time, Pallas kernels for 0%

profile of v3, /device:TPU:1, one launch (start us, length us, event | category | flops | bytes accessed | tf_op | source)
XLA Modules:
  0.0 196.0 jit_solution(12983949417677225075)
XLA Ops:
  7.3 7.8 %collective-permute-start = (bf16[64,4096]{1,0:T(8,128)(2,1)}, bf16[64,4096]{1,0:T(8,128)(2,1)S(1)}, u32[]{:S(2)}, u32[]{:S(2)}) collective-permute-start(bf16[64,4096]{1,0:T(8,128)(2,1)} %param.11), channel_id=1, source_target_pairs={{0,1},{1,0},{2,3},{3,2},{4,5},{5,4},{6,7},{7,6},{8,9},{9,8},{10,11... | collective-permute-start | bytes 1572872 | tf_op jit(solution)/shard_map/ppermute | solution.py:122
  19.9 8.7 %collective-permute-done = bf16[64,4096]{1,0:T(8,128)(2,1)S(1)} collective-permute-done((bf16[64,4096]{1,0:T(8,128)(2,1)}, bf16[64,4096]{1,0:T(8,128)(2,1)S(1)}, u32[]{:S(2)}, u32[]{:S(2)}) %collective-permute-start) | collective-permute-done | bytes 524320 | tf_op jit(solution)/shard_map/ppermute | solution.py:122
  28.6 5.1 %collective-permute-start.3 = (bf16[64,4096]{1,0:T(8,128)(2,1)S(1)}, bf16[64,4096]{1,0:T(8,128)(2,1)}, u32[]{:S(2)}, u32[]{:S(2)}) collective-permute-start(bf16[64,4096]{1,0:T(8,128)(2,1)S(1)} %collective-permute-done), channel_id=1, source_target_pairs={{0,6},{2,0},{4,2},{1,7},{3,1},{5,3},{8,14},{10,8},{12,10},{9,15},{... | collective-permute-start | bytes 1572872 | tf_op jit(solution)/shard_map/ppermute | solution.py:185
  33.7 3.0 %collective-permute-start.2 = (bf16[64,4096]{1,0:T(8,128)(2,1)S(1)}, bf16[64,4096]{1,0:T(8,128)(2,1)}, u32[]{:S(2)}, u32[]{:S(2)}) collective-permute-start(bf16[64,4096]{1,0:T(8,128)(2,1)S(1)} %collective-permute-done), channel_id=1, source_target_pairs={{0,4},{2,6},{4,0},{1,5},{3,7},{5,1},{8,12},{10,14},{12,8},{9,13},{... | collective-permute-start | bytes 1572872 | tf_op jit(solution)/shard_map/ppermute | solution.py:185
  36.7 2.3 %collective-permute-start.1 = (bf16[64,4096]{1,0:T(8,128)(2,1)S(1)}, bf16[64,4096]{1,0:T(8,128)(2,1)}, u32[]{:S(2)}, u32[]{:S(2)}) collective-permute-start(bf16[64,4096]{1,0:T(8,128)(2,1)S(1)} %collective-permute-done), channel_id=1, source_target_pairs={{0,2},{2,4},{4,6},{1,3},{3,5},{5,7},{8,10},{10,12},{12,14},{9,11},... | collective-permute-start | bytes 1572872 | tf_op jit(solution)/shard_map/ppermute | solution.py:185
  39.1 16.9 %all-gather.3.cloned.1.call-done = bf16[256,4096]{1,0:T(8,128)(2,1)} async-done(((bf16[64,4096]{1,0:T(8,128)(2,1)}), bf16[256,4096]{1,0:T(8,128)(2,1)}) %all-gather.3.cloned.1.call-update) | async-done | bytes 2097168 | tf_op jit(solution)/shard_map/all_gather | solution.py:181
  55.9 1.5 slice_dynamic-update-slice_fusion
  57.5 7.2 %collective-permute-done.1 = bf16[64,4096]{1,0:T(8,128)(2,1)} collective-permute-done((bf16[64,4096]{1,0:T(8,128)(2,1)S(1)}, bf16[64,4096]{1,0:T(8,128)(2,1)}, u32[]{:S(2)}, u32[]{:S(2)}) %collective-permute-start.1) | collective-permute-done | bytes 524320 | tf_op jit(solution)/shard_map/ppermute | solution.py:185
  65.8 1.1 constant_dynamic-update-slice_fusion.1
  68.6 1.1 fusion.3
  69.8 2.1 %fusion.6 = bf16[448,4096]{1,0:T(8,128)(2,1)S(1)} fusion(bf16[448,4096]{1,0:T(8,128)(2,1)S(1)} %constant_dynamic-update-slice_fusion, f32[4096]{0:T(1024)S(1)} %copy-done.3, f32[4096]{0:T(1024)S(1)} %copy-done.4, f32[448]{0:T(512)S(1)} %add_rsqrt_fusion, f32[448]{0:T(512)S(1)} %broadcast_multiply_fusion), kind=kLoop, calls=%fused_computation.8 | loop fusion | flops 11010048 | bytes 7376384 | tf_op jit(solution)/shard_map/convert_element_type | solution.py:26
  71.9 1.8 fusion.11
  73.7 1.3 fusion.63
  75.3 1.3 fusion.62
  77.2 2.1 %fusion.61 = (f32[2,448]{1,0:T(2,128)S(1)}, f32[2,448,448]{1,2,0:T(8,128)}) fusion(pred[448,448]{0,1:T(8,128)(4,1)S(1)} %broadcast_compare_fusion, bf16[448,2,128]{0,2,1:T(8,128)(2,1)S(1)} %get-tuple-element.17, bf16[448,2,128]{0,2,1:T(8,128)(2,1)S(1)} %get-tuple-element.16), kind=kOutput, calls=%fused_computation.126 | convolution fusion | flops 104366528 | bytes 2268672 | tf_op jit(solution)/shard_map/sub | solution.py:78
  79.3 2.1 %fusion.10 = bf16[2,56,8,128]{3,2,1,0:T(8,128)(2,1)S(1)} fusion(f32[2,448,448]{1,2,0:T(8,128)} %get-tuple-element.29, f32[2,448]{1,0:T(2,128)S(1)} %get-tuple-element.28, bf16[56,2,8,128]{3,2,1,0:T(8,128)(2,1)} %fusion.11), kind=kOutput, calls=%fused_computation.21 | convolution fusion | flops 103677952 | bytes 2067968 | tf_op jit(solution)/shard_map/hqk,khd->qhd/dot_general | solution.py:107
  81.5 2.7 %convolution_convert_fusion = bf16[328,4096]{1,0:T(8,128)(2,1)} fusion(bf16[256,4096]{1,0:T(8,128)(2,1)S(1)} %copy-done, s32[328]{0:T(512)S(1)} %get-tuple-element.8, bf16[2,56,8,128]{3,2,1,0:T(8,128)(2,1)S(1)} %fusion.10), kind=kOutput, calls=%fused_computation.9 | convolution fusion | flops 764675584 | bytes 5014816 | tf_op jit(solution)/shard_map/dot_general | solution.py:232
  84.2 3.2 %fusion.59 = (bf16[164,4096]{1,0:T(8,128)(2,1)}, bf16[164,4096]{1,0:T(8,128)(2,1)S(1)}) fusion(bf16[328,4096]{1,0:T(8,128)(2,1)} %convolution_convert_fusion), kind=kLoop, calls=%fused_computation.124 | loop fusion | bytes 5373952 | tf_op jit(solution)/shard_map/slice | solution.py:249
  88.5 2.3 %collective-permute-start.4 = (bf16[164,1024]{1,0:T(8,128)(2,1)}, bf16[164,1024]{1,0:T(8,128)(2,1)}, u32[]{:S(2)}, u32[]{:S(2)}) collective-permute-start(bf16[164,1024]{1,0:T(8,128)(2,1)} %get-tuple-element.11), channel_id=1, source_target_pairs={{0,2},{2,4},{4,6},{6,0},{1,3},{3,5},{5,7},{7,1},{8,10},{10,12},{12... | collective-permute-start | bytes 1007624 | tf_op jit(solution)/shard_map/ppermute | solution.py:257
  90.8 1.7 collective-permute-start.6
  92.5 1.7 collective-permute-start.5
  94.2 5.9 %collective-permute-done.4 = bf16[164,1024]{1,0:T(8,128)(2,1)} collective-permute-done((bf16[164,1024]{1,0:T(8,128)(2,1)}, bf16[164,1024]{1,0:T(8,128)(2,1)}, u32[]{:S(2)}, u32[]{:S(2)}) %collective-permute-start.4) | collective-permute-done | bytes 335904 | tf_op jit(solution)/shard_map/ppermute | solution.py:257
  100.1 8.7 %collective-permute-done.5 = bf16[164,1024]{1,0:T(8,128)(2,1)} collective-permute-done((bf16[164,1024]{1,0:T(8,128)(2,1)}, bf16[164,1024]{1,0:T(8,128)(2,1)}, u32[]{:S(2)}, u32[]{:S(2)}) %collective-permute-start.5) | collective-permute-done | bytes 335904 | tf_op jit(solution)/shard_map/ppermute | solution.py:257
  108.9 2.2 %add_convert_fusion = bf16[164,1024]{1,0:T(8,128)(2,1)} fusion(bf16[164,1024]{1,0:T(8,128)(2,1)} %collective-permute-done.6, bf16[164,1024]{1,0:T(8,128)(2,1)} %collective-permute-done.5, bf16[164,1024]{1,0:T(8,128)(2,1)} %collective-permute-done.4, bf16[164,4096]{1,0:T(8,128)(2,1)S(1)} %get-tuple-element.10, s32[]{:T(128)S(6)} %select_n.222), kind=kLoop, calls=%fused_computation.28 | loop fusion | flops 1343488 | bytes 1679364 | tf_op jit(solution)/shard_map/convert_element_type | solution.py:259
  111.0 10.6 %reduce-scatter.2.cloned.1.call-done = bf16[164,1024]{1,0:T(8,128)(2,1)} async-done(((bf16[164,4096]{1,0:T(8,128)(2,1)}), bf16[164,1024]{1,0:T(8,128)(2,1)}) %reduce-scatter.2.cloned.1.call-update) | async-done | bytes 335888 | tf_op jit(solution)/shard_map/reduce_scatter | solution.py:249
  121.7 1.2 pad_maximum_fusion
  125.1 4.3 %collective-permute-start.7 = (bf16[324,512]{1,0:T(8,128)(2,1)S(1)}, bf16[324,512]{1,0:T(8,128)(2,1)S(1)}, u32[]{:S(2)}, u32[]{:S(2)}) collective-permute-start(bf16[324,512]{1,0:T(8,128)(2,1)S(1)} %select_bitcast_fusion), channel_id=1, source_target_pairs={{0,1},{1,0},{2,3},{3,2},{4,5},{5,4},{6,7},{7,6},{8,9},{9,8},{10,11... | collective-permute-start | bytes 995336 | tf_op jit(solution)/shard_map/ppermute | solution.py:122
  130.2 6.8 %collective-permute-done.7 = bf16[324,512]{1,0:T(8,128)(2,1)S(1)} collective-permute-done((bf16[324,512]{1,0:T(8,128)(2,1)S(1)}, bf16[324,512]{1,0:T(8,128)(2,1)S(1)}, u32[]{:S(2)}, u32[]{:S(2)}) %collective-permute-start.7) | collective-permute-done | bytes 331808 | tf_op jit(solution)/shard_map/ppermute | solution.py:122
  137.0 1.7 fusion.9
  139.7 16.8 %all-to-all-start = ((bf16[32,48,128]{2,1,0:T(8,128)(2,1)}), bf16[32,48,128]{2,1,0:T(8,128)(2,1)S(1)}, u32[]{:S(2)}, u32[]{:S(2)}) async-start(bf16[32,48,128]{2,1,0:T(8,128)(2,1)} %bitcast.12), calls=%async_computation.1 | async-start | bytes 786432 | tf_op jit(solution)/shard_map/all_to_all | solution.py:145
  156.7 13.9 %all-to-all-done = bf16[32,48,128]{2,1,0:T(8,128)(2,1)S(1)} async-done(((bf16[32,48,128]{2,1,0:T(8,128)(2,1)}), bf16[32,48,128]{2,1,0:T(8,128)(2,1)S(1)}, u32[]{:S(2)}, u32[]{:S(2)}) %all-to-all-start) | async-done | bytes 393248 | tf_op jit(solution)/shard_map/all_to_all | solution.py:145
  170.8 17.5 %all_to_all.10 = bf16[32,48,128]{2,1,0:T(8,128)(2,1)S(1)} all-to-all(bf16[32,48,128]{2,1,0:T(8,128)(2,1)S(1)} %fusion.21), channel_id=1, replica_groups=mesh['x'=4,'zl'=4,'c'=2,'y'=4,'zh'=2] {'x','zl','c'}, dimensions={0} | all-to-all | bytes 786432 | tf_op jit(solution)/shard_map/all_to_all | solution.py:147
  (70 shorter events, 13.9 us)
Async XLA Ops:
  6.5 74.9 %copy-start = (bf16[256,4096]{1,0:T(8,128)(2,1)S(1)}, bf16[256,4096]{1,0:T(8,128)(2,1)}, u32[]{:S(2)}) copy-start(bf16[256,4096]{1,0:T(8,128)(2,1)} %param.17) | copy-start | bytes 6291460
  6.5 49.4 %all-gather.3.cloned.1.call-start = ((), (), s32[]{:S(2)}) async-start(), calls=%async_computation.4 | async-start | bytes 2621440 | tf_op jit(solution)/shard_map/all_gather | solution.py:181
  7.3 114.4 %reduce-scatter.2.cloned.1.call-start = ((), (), s32[]{:S(2)}) async-start(), calls=%async_computation.3 | async-start | bytes 1720320 | tf_op jit(solution)/shard_map/reduce_scatter | solution.py:249
  7.3 21.3 %collective-permute-start = (bf16[64,4096]{1,0:T(8,128)(2,1)}, bf16[64,4096]{1,0:T(8,128)(2,1)S(1)}, u32[]{:S(2)}, u32[]{:S(2)}) collective-permute-start(bf16[64,4096]{1,0:T(8,128)(2,1)} %param.11), channel_id=1, source_target_pairs={{0,1},{1,0},{2,3},{3,2},{4,5},{5,4},{6,7},{7,6},{8,9},{9,8},{10,11... | collective-permute-start | bytes 1572872 | tf_op jit(solution)/shard_map/ppermute | solution.py:122
  28.6 38.3 %collective-permute-start.3 = (bf16[64,4096]{1,0:T(8,128)(2,1)S(1)}, bf16[64,4096]{1,0:T(8,128)(2,1)}, u32[]{:S(2)}, u32[]{:S(2)}) collective-permute-start(bf16[64,4096]{1,0:T(8,128)(2,1)S(1)} %collective-permute-done), channel_id=1, source_target_pairs={{0,6},{2,0},{4,2},{1,7},{3,1},{5,3},{8,14},{10,8},{12,10},{9,15},{... | collective-permute-start | bytes 1572872 | tf_op jit(solution)/shard_map/ppermute | solution.py:185
  33.7 32.1 %collective-permute-start.2 = (bf16[64,4096]{1,0:T(8,128)(2,1)S(1)}, bf16[64,4096]{1,0:T(8,128)(2,1)}, u32[]{:S(2)}, u32[]{:S(2)}) collective-permute-start(bf16[64,4096]{1,0:T(8,128)(2,1)S(1)} %collective-permute-done), channel_id=1, source_target_pairs={{0,4},{2,6},{4,0},{1,5},{3,7},{5,1},{8,12},{10,14},{12,8},{9,13},{... | collective-permute-start | bytes 1572872 | tf_op jit(solution)/shard_map/ppermute | solution.py:185
  36.7 28.0 %collective-permute-start.1 = (bf16[64,4096]{1,0:T(8,128)(2,1)S(1)}, bf16[64,4096]{1,0:T(8,128)(2,1)}, u32[]{:S(2)}, u32[]{:S(2)}) collective-permute-start(bf16[64,4096]{1,0:T(8,128)(2,1)S(1)} %collective-permute-done), channel_id=1, source_target_pairs={{0,2},{2,4},{4,6},{1,3},{3,5},{5,7},{8,10},{10,12},{12,14},{9,11},... | collective-permute-start | bytes 1572872 | tf_op jit(solution)/shard_map/ppermute | solution.py:185
  68.0 1.8 copy-start.1
  68.0 1.8 copy-start.3
  68.0 1.8 copy-start.4
  69.8 2.1 %copy-start.6 = (bf16[4096,256]{1,0:T(8,128)(2,1)S(1)}, bf16[4096,256]{1,0:T(8,128)(2,1)}, u32[]{:S(2)}) copy-start(bf16[4096,256]{1,0:T(8,128)(2,1)} %param.16) | copy-start | bytes 6291460
  71.9 1.8 copy-start.7
  73.7 1.6 copy-start.8
  88.5 11.7 %collective-permute-start.4 = (bf16[164,1024]{1,0:T(8,128)(2,1)}, bf16[164,1024]{1,0:T(8,128)(2,1)}, u32[]{:S(2)}, u32[]{:S(2)}) collective-permute-start(bf16[164,1024]{1,0:T(8,128)(2,1)} %get-tuple-element.11), channel_id=1, source_target_pairs={{0,2},{2,4},{4,6},{6,0},{1,3},{3,5},{5,7},{7,1},{8,10},{10,12},{12... | collective-permute-start | bytes 1007624 | tf_op jit(solution)/shard_map/ppermute | solution.py:257
  90.8 9.4 %collective-permute-start.6 = (bf16[164,1024]{1,0:T(8,128)(2,1)}, bf16[164,1024]{1,0:T(8,128)(2,1)}, u32[]{:S(2)}, u32[]{:S(2)}) collective-permute-start(bf16[164,1024]{1,0:T(8,128)(2,1)} %get-tuple-element.12), channel_id=1, source_target_pairs={{0,6},{2,0},{4,2},{6,4},{1,7},{3,1},{5,3},{7,5},{8,14},{10,8},{12,... | collective-permute-start | bytes 1007624 | tf_op jit(solution)/shard_map/ppermute | solution.py:257
  92.5 16.4 %collective-permute-start.5 = (bf16[164,1024]{1,0:T(8,128)(2,1)}, bf16[164,1024]{1,0:T(8,128)(2,1)}, u32[]{:S(2)}, u32[]{:S(2)}) collective-permute-start(bf16[164,1024]{1,0:T(8,128)(2,1)} %get-tuple-element.13), channel_id=1, source_target_pairs={{0,4},{2,6},{4,0},{6,2},{1,5},{3,7},{5,1},{7,3},{8,12},{10,14},{12... | collective-permute-start | bytes 1007624 | tf_op jit(solution)/shard_map/ppermute | solution.py:257
  111.0 26.0 %copy-start.9 = (f32[512]{0:T(512)S(1)}, f32[512]{0:T(512)}, u32[]{:S(2)}) copy-start(f32[512]{0:T(512)} %param.18) | copy-start | bytes 6148
  124.2 0.8 copy-start.2
  124.2 32.4 %copy-start.5 = (s32[32,1]{0,1:T(1,128)S(1)}, s32[32,1]{0,1:T(1,128)}, u32[]{:S(2)}) copy-start(s32[32,1]{0,1:T(1,128)} %param.21) | copy-start | bytes 388
  125.1 11.9 %collective-permute-start.7 = (bf16[324,512]{1,0:T(8,128)(2,1)S(1)}, bf16[324,512]{1,0:T(8,128)(2,1)S(1)}, u32[]{:S(2)}, u32[]{:S(2)}) collective-permute-start(bf16[324,512]{1,0:T(8,128)(2,1)S(1)} %select_bitcast_fusion), channel_id=1, source_target_pairs={{0,1},{1,0},{2,3},{3,2},{4,5},{5,4},{6,7},{7,6},{8,9},{9,8},{10,11... | collective-permute-start | bytes 995336 | tf_op jit(solution)/shard_map/ppermute | solution.py:122
  139.7 30.9 %all-to-all-start = ((bf16[32,48,128]{2,1,0:T(8,128)(2,1)}), bf16[32,48,128]{2,1,0:T(8,128)(2,1)S(1)}, u32[]{:S(2)}, u32[]{:S(2)}) async-start(bf16[32,48,128]{2,1,0:T(8,128)(2,1)} %bitcast.12), calls=%async_computation.1 | async-start | bytes 786432 | tf_op jit(solution)/shard_map/all_to_all | solution.py:145
Sparse Core Ops, SparseCore 0:
  9.1 46.7 all-gather.2
  87.5 34.0 reduce-scatter.1

commit v4 on v2

--- a/solution.py
+++ b/solution.py
@@ -244,7 +244,17 @@
         preferred_element_type=jnp.float32,
     )
 
-    quarter = lax.psum_scatter(partial_sum, "y", scatter_dimension=1, tiled=True)
+    quarter_cols = feat_cols * lax.axis_size("zh")
+    quarter = lax.dynamic_slice_in_dim(
+        partial_sum, y_index * quarter_cols, quarter_cols, axis=1
+    ).astype(jnp.float32)
+    for by in range(1, y_count):
+        chunk = lax.dynamic_slice_in_dim(
+            partial_sum, ((y_index + by) % y_count) * quarter_cols, quarter_cols, axis=1
+        )
+        moved = lax.ppermute(chunk, "y", [(src, (src + by) % y_count) for src in range(y_count)])
+        quarter = quarter + moved.astype(jnp.float32)
+    quarter = quarter.astype(jnp.bfloat16)
     split = quarter.reshape(MERGE_PAD, 2, feat_cols)[: source_rows.shape[0]]
     mine = jnp.where(zh == 0, split[:, 0], split[:, 1])
     theirs = jnp.where(zh == 0, split[:, 1], split[:, 0])

time: 202 us -> 197 us (0.975)
  waiting for transfers between devices: 98.4 us -> 85 us
  starting transfers between devices: 37.1 us -> 42.7 us
  other arithmetic: 8.18 us -> 10.4 us
    reduce_scatter x1 -> x0, waiting for transfers between devices: 42.6 us -> none  [body(): lax.psum_scatter(partial_sum, 'y', scatter_dimension=1, tiled=True)]
    ppermute x0 -> x3, waiting for transfers between devices: none -> 28.2 us  [body(): lax.ppermute(chunk, 'y', [(src, (src + by) % y_count) for src in range(y_...]
    ppermute x0 -> x3, starting transfers between devices: none -> 5.75 us  [body(): lax.ppermute(chunk, 'y', [(src, (src + by) % y_count) for src in range(y_...]
    ppermute x2, starting transfers between devices: 13.4 us -> 9.14 us  [swap_pair(): return lax.ppermute(array, 'zh', [(0, 1), (1, 0)])]
    all_to_all x1, starting transfers between devices: 13.2 us -> 17.4 us  [shift_by_exchange(): lax.all_to_all(flat.reshape(count, rows, lanes), DP_AXES, 0, 0, tiled=True)]
    dynamic_slice x0 -> x1, local copies, waits for them, and re-layouts: none -> 2.58 us  [body(): lax.dynamic_slice_in_dim(partial_sum, (y_index + by) % y_count * quarter_...]
    convert_element_type x0 -> x1, other arithmetic: none -> 2.19 us  [body(): quarter = quarter.astype(jnp.bfloat16)]
  transfers between devices with their start and end apart: 8 -> 10, of which waited for: 6 -> 7; matrix products, arithmetic and copies ran while one was open for 4% -> 4% of each run, Pallas kernels for 0% -> 0%
where the time goes in v4:
time: 197 us; the launch traced here: 196 us
  waiting for transfers between devices  85 us (43%)
  starting transfers between devices  42.7 us (22%)
  blocking collectives  17.5 us (9%)
  between operations  15.3 us (8%)
  matrix products  13.1 us (7%)
  local copies, waits for them, and re-layouts  12.3 us (6%)
  other arithmetic  10.4 us (5%)
    ppermute x3, waiting for transfers between devices, body(): lax.ppermute(chunk, 'y', [(src, (src + by) % y_count) for src in range(y_...  28.2 us
    ppermute x2, waiting for transfers between devices, swap_pair(): return lax.ppermute(array, 'zh', [(0, 1), (1, 0)])  18 us
    all_to_all x1, blocking collectives, shift_by_exchange(): back = lax.all_to_all(rolled, DP_AXES, 0, 0, tiled=True)  17.5 us
    all_to_all x1, starting transfers between devices, shift_by_exchange(): lax.all_to_all(flat.reshape(count, rows, lanes), DP_AXES, 0, 0, tiled=True)  17.4 us
    all_gather x1, waiting for transfers between devices, body(): own_blocks = lax.all_gather(stream_rows, 'y', axis=0, tiled=False)  16.9 us
    all_to_all x1, waiting for transfers between devices, shift_by_exchange(): lax.all_to_all(flat.reshape(count, rows, lanes), DP_AXES, 0, 0, tiled=True)  13.9 us
    ppermute x3, starting transfers between devices, body(): lax.ppermute(partner, 'y', [(src, (src + by) % y_count) for src in range(...  10.4 us
    ppermute x2, starting transfers between devices, swap_pair(): return lax.ppermute(array, 'zh', [(0, 1), (1, 0)])  9.14 us
  transfers between devices with their start and end apart: 10, of which 7 were waited for; matrix products, arithmetic and copies ran while one was open for 4% of the time, Pallas kernels for 0%

profile of v4, /device:TPU:1, one launch (start us, length us, event | category | flops | bytes accessed | tf_op | source)
XLA Modules:
  0.0 196.1 jit_solution(5844955158245776527)
XLA Ops:
  7.3 7.8 %collective-permute-start = (bf16[64,4096]{1,0:T(8,128)(2,1)}, bf16[64,4096]{1,0:T(8,128)(2,1)S(1)}, u32[]{:S(2)}, u32[]{:S(2)}) collective-permute-start(bf16[64,4096]{1,0:T(8,128)(2,1)} %param.11), channel_id=1, source_target_pairs={{0,1},{1,0},{2,3},{3,2},{4,5},{5,4},{6,7},{7,6},{8,9},{9,8},{10,11... | collective-permute-start | bytes 1572872 | tf_op jit(solution)/shard_map/ppermute | solution.py:122
  19.9 8.7 %collective-permute-done = bf16[64,4096]{1,0:T(8,128)(2,1)S(1)} collective-permute-done((bf16[64,4096]{1,0:T(8,128)(2,1)}, bf16[64,4096]{1,0:T(8,128)(2,1)S(1)}, u32[]{:S(2)}, u32[]{:S(2)}) %collective-permute-start) | collective-permute-done | bytes 524320 | tf_op jit(solution)/shard_map/ppermute | solution.py:122
  28.6 5.1 %collective-permute-start.3 = (bf16[64,4096]{1,0:T(8,128)(2,1)S(1)}, bf16[64,4096]{1,0:T(8,128)(2,1)}, u32[]{:S(2)}, u32[]{:S(2)}) collective-permute-start(bf16[64,4096]{1,0:T(8,128)(2,1)S(1)} %collective-permute-done), channel_id=1, source_target_pairs={{0,6},{2,0},{4,2},{1,7},{3,1},{5,3},{8,14},{10,8},{12,10},{9,15},{... | collective-permute-start | bytes 1572872 | tf_op jit(solution)/shard_map/ppermute | solution.py:185
  33.6 3.0 %collective-permute-start.2 = (bf16[64,4096]{1,0:T(8,128)(2,1)S(1)}, bf16[64,4096]{1,0:T(8,128)(2,1)}, u32[]{:S(2)}, u32[]{:S(2)}) collective-permute-start(bf16[64,4096]{1,0:T(8,128)(2,1)S(1)} %collective-permute-done), channel_id=1, source_target_pairs={{0,4},{2,6},{4,0},{1,5},{3,7},{5,1},{8,12},{10,14},{12,8},{9,13},{... | collective-permute-start | bytes 1572872 | tf_op jit(solution)/shard_map/ppermute | solution.py:185
  36.7 2.3 %collective-permute-start.1 = (bf16[64,4096]{1,0:T(8,128)(2,1)S(1)}, bf16[64,4096]{1,0:T(8,128)(2,1)}, u32[]{:S(2)}, u32[]{:S(2)}) collective-permute-start(bf16[64,4096]{1,0:T(8,128)(2,1)S(1)} %collective-permute-done), channel_id=1, source_target_pairs={{0,2},{2,4},{4,6},{1,3},{3,5},{5,7},{8,10},{10,12},{12,14},{9,11},... | collective-permute-start | bytes 1572872 | tf_op jit(solution)/shard_map/ppermute | solution.py:185
  39.0 16.9 %all-gather.3.cloned.1.call-done = bf16[256,4096]{1,0:T(8,128)(2,1)} async-done(((bf16[64,4096]{1,0:T(8,128)(2,1)}), bf16[256,4096]{1,0:T(8,128)(2,1)}) %all-gather.3.cloned.1.call-update) | async-done | bytes 2097168 | tf_op jit(solution)/shard_map/all_gather | solution.py:181
  55.9 1.5 slice_dynamic-update-slice_fusion
  57.5 7.2 %collective-permute-done.1 = bf16[64,4096]{1,0:T(8,128)(2,1)} collective-permute-done((bf16[64,4096]{1,0:T(8,128)(2,1)S(1)}, bf16[64,4096]{1,0:T(8,128)(2,1)}, u32[]{:S(2)}, u32[]{:S(2)}) %collective-permute-start.1) | collective-permute-done | bytes 524320 | tf_op jit(solution)/shard_map/ppermute | solution.py:185
  64.7 1.1 constant_dynamic-update-slice_fusion.2
  65.8 1.1 constant_dynamic-update-slice_fusion.1
  66.9 1.1 constant_dynamic-update-slice_fusion
  68.6 1.1 fusion.3
  69.8 2.1 %fusion.6 = bf16[448,4096]{1,0:T(8,128)(2,1)S(1)} fusion(bf16[448,4096]{1,0:T(8,128)(2,1)S(1)} %constant_dynamic-update-slice_fusion, f32[4096]{0:T(1024)S(1)} %copy-done.3, f32[4096]{0:T(1024)S(1)} %copy-done.4, f32[448]{0:T(512)S(1)} %add_rsqrt_fusion, f32[448]{0:T(512)S(1)} %broadcast_multiply_fusion), kind=kLoop, calls=%fused_computation.8 | loop fusion | flops 11010048 | bytes 7376384 | tf_op jit(solution)/shard_map/convert_element_type | solution.py:26
  71.9 1.8 fusion.11
  73.7 1.3 fusion.62
  75.3 1.3 fusion.61
  77.1 2.1 %fusion.60 = (f32[2,448]{1,0:T(2,128)S(1)}, f32[2,448,448]{1,2,0:T(8,128)}) fusion(pred[448,448]{0,1:T(8,128)(4,1)S(1)} %broadcast_compare_fusion, bf16[448,2,128]{0,2,1:T(8,128)(2,1)S(1)} %get-tuple-element.15, bf16[448,2,128]{0,2,1:T(8,128)(2,1)S(1)} %get-tuple-element.14), kind=kOutput, calls=%fused_computation.124 | convolution fusion | flops 104366528 | bytes 2268672 | tf_op jit(solution)/shard_map/sub | solution.py:78
  79.3 2.1 %fusion.10 = bf16[2,56,8,128]{3,2,1,0:T(8,128)(2,1)S(1)} fusion(f32[2,448,448]{1,2,0:T(8,128)} %get-tuple-element.27, f32[2,448]{1,0:T(2,128)S(1)} %get-tuple-element.26, bf16[56,2,8,128]{3,2,1,0:T(8,128)(2,1)} %fusion.11), kind=kOutput, calls=%fused_computation.22 | convolution fusion | flops 103677952 | bytes 2067968 | tf_op jit(solution)/shard_map/hqk,khd->qhd/dot_general | solution.py:107
  81.4 2.7 %convolution_convert_fusion = bf16[328,4096]{1,0:T(8,128)(2,1)} fusion(bf16[256,4096]{1,0:T(8,128)(2,1)S(1)} %copy-done, s32[328]{0:T(512)S(1)} %get-tuple-element.8, bf16[2,56,8,128]{3,2,1,0:T(8,128)(2,1)S(1)} %fusion.10), kind=kOutput, calls=%fused_computation.9 | convolution fusion | flops 764675584 | bytes 5014816 | tf_op jit(solution)/shard_map/dot_general | solution.py:232
  84.1 2.6 %constant_dynamic-slice_fusion.2 = (bf16[328,1024]{1,0:T(8,128)(2,1)}, bf16[328,1024]{1,0:T(8,128)(2,1)S(1)}, bf16[328,1024]{1,0:T(8,128)(2,1)S(1)}) fusion(bf16[328,4096]{1,0:T(8,128)(2,1)} %convolution_convert_fusion, s32[]{:T(128)S(6)} %select_n.224, s32[]{:T(128)S(6)} %select_n.228, s32[]{:T(128)S(6)} %select_n.226), kind=kLoop, calls=%fused_computation.101 | loop fusion | bytes 4030476 | tf_op jit(solution)/shard_map/dynamic_slice | solution.py:252
  86.7 2.3 %collective-permute-start.4 = (bf16[328,1024]{1,0:T(8,128)(2,1)}, bf16[328,1024]{1,0:T(8,128)(2,1)}, u32[]{:S(2)}, u32[]{:S(2)}) collective-permute-start(bf16[328,1024]{1,0:T(8,128)(2,1)} %get-tuple-element.9), channel_id=1, source_target_pairs={{0,2},{2,4},{4,6},{6,0},{1,3},{3,5},{5,7},{7,1},{8,10},{10,12},{12... | collective-permute-start | bytes 2015240 | tf_op jit(solution)/shard_map/ppermute | solution.py:255
  89.0 1.7 collective-permute-start.6
  90.7 1.8 collective-permute-start.5
  92.5 13.0 %collective-permute-done.4 = bf16[328,1024]{1,0:T(8,128)(2,1)} collective-permute-done((bf16[328,1024]{1,0:T(8,128)(2,1)}, bf16[328,1024]{1,0:T(8,128)(2,1)}, u32[]{:S(2)}, u32[]{:S(2)}) %collective-permute-start.4) | collective-permute-done | bytes 671776 | tf_op jit(solution)/shard_map/ppermute | solution.py:255
  105.4 15.3 %collective-permute-done.5 = bf16[328,1024]{1,0:T(8,128)(2,1)} collective-permute-done((bf16[328,1024]{1,0:T(8,128)(2,1)S(1)}, bf16[328,1024]{1,0:T(8,128)(2,1)}, u32[]{:S(2)}, u32[]{:S(2)}) %collective-permute-start.5) | collective-permute-done | bytes 671776 | tf_op jit(solution)/shard_map/ppermute | solution.py:255
  120.7 2.2 %add_convert_fusion = bf16[324,1024]{1,0:T(8,128)(2,1)S(1)} fusion(bf16[328,1024]{1,0:T(8,128)(2,1)} %collective-permute-done.6, bf16[328,1024]{1,0:T(8,128)(2,1)} %collective-permute-done.5, bf16[328,1024]{1,0:T(8,128)(2,1)} %collective-permute-done.4, bf16[328,4096]{1,0:T(8,128)(2,1)} %convolution_convert_fusion, s32[]{:T(128)S(6)} %select_n.222), kind=kLoop, calls=%fused_computation.15 | loop fusion | flops 2654208 | bytes 3317764 | tf_op jit(solution)/shard_map/convert_element_type | solution.py:257
  125.1 1.3 collective-permute-start.7
  127.3 9.3 %collective-permute-done.7 = bf16[324,512]{1,0:T(8,128)(2,1)S(1)} collective-permute-done((bf16[324,512]{1,0:T(8,128)(2,1)S(1)}, bf16[324,512]{1,0:T(8,128)(2,1)S(1)}, u32[]{:S(2)}, u32[]{:S(2)}) %collective-permute-start.7) | collective-permute-done | bytes 331808 | tf_op jit(solution)/shard_map/ppermute | solution.py:122
  136.7 1.7 fusion.9
  139.3 17.4 %all-to-all-start = ((bf16[32,48,128]{2,1,0:T(8,128)(2,1)}), bf16[32,48,128]{2,1,0:T(8,128)(2,1)S(1)}, u32[]{:S(2)}, u32[]{:S(2)}) async-start(bf16[32,48,128]{2,1,0:T(8,128)(2,1)} %bitcast.12), calls=%async_computation | async-start | bytes 786432 | tf_op jit(solution)/shard_map/all_to_all | solution.py:145
  156.8 13.9 %all-to-all-done = bf16[32,48,128]{2,1,0:T(8,128)(2,1)S(1)} async-done(((bf16[32,48,128]{2,1,0:T(8,128)(2,1)}), bf16[32,48,128]{2,1,0:T(8,128)(2,1)S(1)}, u32[]{:S(2)}, u32[]{:S(2)}) %all-to-all-start) | async-done | bytes 393248 | tf_op jit(solution)/shard_map/all_to_all | solution.py:145
  170.9 17.5 %all_to_all.10 = bf16[32,48,128]{2,1,0:T(8,128)(2,1)S(1)} all-to-all(bf16[32,48,128]{2,1,0:T(8,128)(2,1)S(1)} %fusion.21), channel_id=1, replica_groups=mesh['x'=4,'zl'=4,'c'=2,'y'=4,'zh'=2] {'x','zl','c'}, dimensions={0} | all-to-all | bytes 786432 | tf_op jit(solution)/shard_map/all_to_all | solution.py:147
  (65 shorter events, 10.7 us)
Async XLA Ops:
  6.5 74.9 %copy-start = (bf16[256,4096]{1,0:T(8,128)(2,1)S(1)}, bf16[256,4096]{1,0:T(8,128)(2,1)}, u32[]{:S(2)}) copy-start(bf16[256,4096]{1,0:T(8,128)(2,1)} %param.17) | copy-start | bytes 6291460
  6.5 49.4 %all-gather.3.cloned.1.call-start = ((), (), s32[]{:S(2)}) async-start(), calls=%async_computation.2 | async-start | bytes 2621440 | tf_op jit(solution)/shard_map/all_gather | solution.py:181
  7.3 21.3 %collective-permute-start = (bf16[64,4096]{1,0:T(8,128)(2,1)}, bf16[64,4096]{1,0:T(8,128)(2,1)S(1)}, u32[]{:S(2)}, u32[]{:S(2)}) collective-permute-start(bf16[64,4096]{1,0:T(8,128)(2,1)} %param.11), channel_id=1, source_target_pairs={{0,1},{1,0},{2,3},{3,2},{4,5},{5,4},{6,7},{7,6},{8,9},{9,8},{10,11... | collective-permute-start | bytes 1572872 | tf_op jit(solution)/shard_map/ppermute | solution.py:122
  28.6 38.3 %collective-permute-start.3 = (bf16[64,4096]{1,0:T(8,128)(2,1)S(1)}, bf16[64,4096]{1,0:T(8,128)(2,1)}, u32[]{:S(2)}, u32[]{:S(2)}) collective-permute-start(bf16[64,4096]{1,0:T(8,128)(2,1)S(1)} %collective-permute-done), channel_id=1, source_target_pairs={{0,6},{2,0},{4,2},{1,7},{3,1},{5,3},{8,14},{10,8},{12,10},{9,15},{... | collective-permute-start | bytes 1572872 | tf_op jit(solution)/shard_map/ppermute | solution.py:185
  33.6 32.1 %collective-permute-start.2 = (bf16[64,4096]{1,0:T(8,128)(2,1)S(1)}, bf16[64,4096]{1,0:T(8,128)(2,1)}, u32[]{:S(2)}, u32[]{:S(2)}) collective-permute-start(bf16[64,4096]{1,0:T(8,128)(2,1)S(1)} %collective-permute-done), channel_id=1, source_target_pairs={{0,4},{2,6},{4,0},{1,5},{3,7},{5,1},{8,12},{10,14},{12,8},{9,13},{... | collective-permute-start | bytes 1572872 | tf_op jit(solution)/shard_map/ppermute | solution.py:185
  36.7 28.0 %collective-permute-start.1 = (bf16[64,4096]{1,0:T(8,128)(2,1)S(1)}, bf16[64,4096]{1,0:T(8,128)(2,1)}, u32[]{:S(2)}, u32[]{:S(2)}) collective-permute-start(bf16[64,4096]{1,0:T(8,128)(2,1)S(1)} %collective-permute-done), channel_id=1, source_target_pairs={{0,2},{2,4},{4,6},{1,3},{3,5},{5,7},{8,10},{10,12},{12,14},{9,11},... | collective-permute-start | bytes 1572872 | tf_op jit(solution)/shard_map/ppermute | solution.py:185
  68.0 1.8 copy-start.1
  68.0 1.8 copy-start.3
  68.0 1.8 copy-start.4
  69.8 2.1 %copy-start.6 = (bf16[4096,256]{1,0:T(8,128)(2,1)S(1)}, bf16[4096,256]{1,0:T(8,128)(2,1)}, u32[]{:S(2)}) copy-start(bf16[4096,256]{1,0:T(8,128)(2,1)} %param.16) | copy-start | bytes 6291460
  71.9 1.8 copy-start.7
  73.7 1.6 copy-start.8
  86.7 18.7 %collective-permute-start.4 = (bf16[328,1024]{1,0:T(8,128)(2,1)}, bf16[328,1024]{1,0:T(8,128)(2,1)}, u32[]{:S(2)}, u32[]{:S(2)}) collective-permute-start(bf16[328,1024]{1,0:T(8,128)(2,1)} %get-tuple-element.9), channel_id=1, source_target_pairs={{0,2},{2,4},{4,6},{6,0},{1,3},{3,5},{5,7},{7,1},{8,10},{10,12},{12... | collective-permute-start | bytes 2015240 | tf_op jit(solution)/shard_map/ppermute | solution.py:255
  89.0 16.4 %collective-permute-start.6 = (bf16[328,1024]{1,0:T(8,128)(2,1)S(1)}, bf16[328,1024]{1,0:T(8,128)(2,1)}, u32[]{:S(2)}, u32[]{:S(2)}) collective-permute-start(bf16[328,1024]{1,0:T(8,128)(2,1)S(1)} %get-tuple-element.10), channel_id=1, source_target_pairs={{0,6},{2,0},{4,2},{6,4},{1,7},{3,1},{5,3},{7,5},{8,14},{10,8},{12,... | collective-permute-start | bytes 2015240 | tf_op jit(solution)/shard_map/ppermute | solution.py:255
  90.7 30.0 %collective-permute-start.5 = (bf16[328,1024]{1,0:T(8,128)(2,1)S(1)}, bf16[328,1024]{1,0:T(8,128)(2,1)}, u32[]{:S(2)}, u32[]{:S(2)}) collective-permute-start(bf16[328,1024]{1,0:T(8,128)(2,1)S(1)} %get-tuple-element.11), channel_id=1, source_target_pairs={{0,4},{2,6},{4,0},{6,2},{1,5},{3,7},{5,1},{7,3},{8,12},{10,14},{12... | collective-permute-start | bytes 2015240 | tf_op jit(solution)/shard_map/ppermute | solution.py:255
  122.9 13.8 %copy-start.9 = (f32[512]{0:T(512)S(1)}, f32[512]{0:T(512)}, u32[]{:S(2)}) copy-start(f32[512]{0:T(512)} %param.18) | copy-start | bytes 6148
  124.2 0.8 copy-start.2
  124.2 32.4 %copy-start.5 = (s32[32,1]{0,1:T(1,128)S(1)}, s32[32,1]{0,1:T(1,128)}, u32[]{:S(2)}) copy-start(s32[32,1]{0,1:T(1,128)} %param.21) | copy-start | bytes 388
  125.1 11.5 %collective-permute-start.7 = (bf16[324,512]{1,0:T(8,128)(2,1)S(1)}, bf16[324,512]{1,0:T(8,128)(2,1)S(1)}, u32[]{:S(2)}, u32[]{:S(2)}) collective-permute-start(bf16[324,512]{1,0:T(8,128)(2,1)S(1)} %select_bitcast_fusion), channel_id=1, source_target_pairs={{0,1},{1,0},{2,3},{3,2},{4,5},{5,4},{6,7},{7,6},{8,9},{9,8},{10,11... | collective-permute-start | bytes 995336 | tf_op jit(solution)/shard_map/ppermute | solution.py:122
  139.3 31.4 %all-to-all-start = ((bf16[32,48,128]{2,1,0:T(8,128)(2,1)}), bf16[32,48,128]{2,1,0:T(8,128)(2,1)S(1)}, u32[]{:S(2)}, u32[]{:S(2)}) async-start(bf16[32,48,128]{2,1,0:T(8,128)(2,1)} %bitcast.12), calls=%async_computation | async-start | bytes 786432 | tf_op jit(solution)/shard_map/all_to_all | solution.py:145
Sparse Core Ops, SparseCore 0:
  9.1 46.7 all-gather.2

commit v5 on v4

--- a/solution.py
+++ b/solution.py
@@ -136,6 +136,22 @@
     return lax.switch(distance, [branch(by) for by in range(count)], block)
 
 
+def scatter_pieces(payload):
+    count = lax.axis_size(DP_AXES)
+    size = payload.size
+    lanes = 128
+    rows = -(-size // (count * lanes))
+    rows = -(-rows // 16) * 16
+    flat = jnp.pad(payload.reshape(-1), (0, count * rows * lanes - size))
+    return lax.all_to_all(flat.reshape(count, rows, lanes), DP_AXES, 0, 0, tiled=True)
+
+
+def gather_pieces(pieces, distance, shape):
+    size = math.prod(shape)
+    back = lax.all_to_all(jnp.roll(pieces, distance, axis=0), DP_AXES, 0, 0, tiled=True)
+    return back.reshape(-1)[:size].reshape(shape)
+
+
 def shift_by_exchange(payload, distance, count):
     size = payload.size
     lanes = 128
@@ -238,11 +254,13 @@
     distance = owners[0, 0] % group_count
 
     feat_index = lax.axis_index("y") * lax.axis_size("zh") + zh
+    keep = jnp.repeat(valid, 4)[:, None]
     residual = jnp.dot(
         one_hot(position_of(source_rows, row_ids), row_count),
         lax.dynamic_slice_in_dim(live_rows, feat_index * feat_cols, feat_cols, axis=1),
         preferred_element_type=jnp.float32,
-    )
+    ).astype(jnp.bfloat16)
+    residual_pieces = scatter_pieces(jnp.where(keep, residual, jnp.zeros_like(residual)))
 
     quarter_cols = feat_cols * lax.axis_size("zh")
     quarter = lax.dynamic_slice_in_dim(
@@ -258,12 +276,16 @@
     split = quarter.reshape(MERGE_PAD, 2, feat_cols)[: source_rows.shape[0]]
     mine = jnp.where(zh == 0, split[:, 0], split[:, 1])
     theirs = jnp.where(zh == 0, split[:, 1], split[:, 0])
-    branch = mine.astype(jnp.float32) + swap_pair(theirs).astype(jnp.float32)
-    updated = (residual + scale_ls * branch).astype(jnp.bfloat16)
-    merged = jnp.where(jnp.repeat(valid, 4)[:, None], updated, jnp.zeros_like(updated))
-    delivered = shift_by_exchange(merged, distance, group_count).reshape(
-        1, CAP, 4, feat_cols
-    )
+    mine_pieces = scatter_pieces(jnp.where(keep, mine, jnp.zeros_like(mine)))
+    theirs = swap_pair(theirs)
+    theirs_pieces = scatter_pieces(jnp.where(keep, theirs, jnp.zeros_like(theirs)))
+    piece_size = mine_pieces.shape[1] * mine_pieces.shape[2]
+    piece_index = lax.axis_index(DP_AXES)
+    cols = (piece_index * piece_size + jnp.arange(piece_size, dtype=jnp.int32)) % feat_cols
+    piece_scale = jnp.take(scale_ls, cols).reshape(mine_pieces.shape[1:])
+    branch = mine_pieces.astype(jnp.float32) + theirs_pieces.astype(jnp.float32)
+    updated = (residual_pieces.astype(jnp.float32) + piece_scale * branch).astype(jnp.bfloat16)
+    delivered = gather_pieces(updated, distance, residual.shape).reshape(1, CAP, 4, feat_cols)
     return delivered[None]
 
 

time: 197 us -> 243 us (1.23)
  local copies, waits for them, and re-layouts: 12.3 us -> 53.2 us
  waiting for transfers between devices: 85 us -> 69.3 us
  starting transfers between devices: 42.7 us -> 56.9 us
  blocking collectives: 17.5 us -> 21.5 us
    gather x0 -> x1, local copies, waits for them, and re-layouts: none -> 38.6 us  [body(): piece_scale = jnp.take(scale_ls, cols).reshape(mine_pieces.shape[1:])]
    ppermute x3, waiting for transfers between devices: 28.2 us -> 13.3 us  [body(): lax.ppermute(chunk, 'y', [(src, (src + by) % y_count) for src in range(y_...]
    all_to_all x1 -> x3, starting transfers between devices: 17.4 us -> 28.1 us  [scatter_pieces(): lax.all_to_all(flat.reshape(count, rows, lanes), DP_AXES, 0, 0, tiled=True)]
    all_to_all x1 -> x3, waiting for transfers between devices: 13.9 us -> 3.98 us  [scatter_pieces(): lax.all_to_all(flat.reshape(count, rows, lanes), DP_AXES, 0, 0, tiled=True)]
    ppermute x2, waiting for transfers between devices: 18 us -> 27.2 us  [swap_pair(): return lax.ppermute(array, 'zh', [(0, 1), (1, 0)])]
    all_to_all x1, blocking collectives: 17.5 us -> 21.5 us  [gather_pieces(): lax.all_to_all(jnp.roll(pieces, distance, axis=0), DP_AXES, 0, 0, tiled=T...]
    ppermute x2, starting transfers between devices: 9.14 us -> 12.6 us  [swap_pair(): return lax.ppermute(array, 'zh', [(0, 1), (1, 0)])]
    unnamed x24 -> x22, local copies, waits for them, and re-layouts: 4.9 us -> 4.09 us
  transfers between devices with their start and end apart: 10 -> 12, of which waited for: 7 -> 6; matrix products, arithmetic and copies ran while one was open for 4% -> 23% of each run, Pallas kernels for 0% -> 0%
where the time goes in v5:
time: 243 us; the launch traced here: 242 us
  waiting for transfers between devices  69.3 us (29%)
  starting transfers between devices  56.9 us (23%)
  local copies, waits for them, and re-layouts  53.2 us (22%)
  blocking collectives  21.5 us (9%)
  between operations  15.4 us (6%)
  matrix products  12.9 us (5%)
  other arithmetic  12.8 us (5%)
    gather x1, local copies, waits for them, and re-layouts, body(): piece_scale = jnp.take(scale_ls, cols).reshape(mine_pieces.shape[1:])  38.6 us
    all_to_all x3, starting transfers between devices, scatter_pieces(): lax.all_to_all(flat.reshape(count, rows, lanes), DP_AXES, 0, 0, tiled=True)  28.1 us
    ppermute x2, waiting for transfers between devices, swap_pair(): return lax.ppermute(array, 'zh', [(0, 1), (1, 0)])  27.2 us
    all_to_all x1, blocking collectives, gather_pieces(): lax.all_to_all(jnp.roll(pieces, distance, axis=0), DP_AXES, 0, 0, tiled=T...  21.5 us
    all_gather x1, waiting for transfers between devices, body(): own_blocks = lax.all_gather(stream_rows, 'y', axis=0, tiled=False)  16.9 us
    ppermute x3, waiting for transfers between devices, body(): lax.ppermute(chunk, 'y', [(src, (src + by) % y_count) for src in range(y_...  13.3 us
    ppermute x2, starting transfers between devices, swap_pair(): return lax.ppermute(array, 'zh', [(0, 1), (1, 0)])  12.6 us
    ppermute x3, starting transfers between devices, body(): lax.ppermute(partner, 'y', [(src, (src + by) % y_count) for src in range(...  10.4 us
  transfers between devices with their start and end apart: 12, of which 6 were waited for; matrix products, arithmetic and copies ran while one was open for 23% of the time, Pallas kernels for 0%

profile of v5, /device:TPU:1, one launch (start us, length us, event | category | flops | bytes accessed | tf_op | source)
XLA Modules:
  0.0 242.0 jit_solution(7449732438716168764)
XLA Ops:
  7.3 7.8 %collective-permute-start = (bf16[64,4096]{1,0:T(8,128)(2,1)}, bf16[64,4096]{1,0:T(8,128)(2,1)S(1)}, u32[]{:S(2)}, u32[]{:S(2)}) collective-permute-start(bf16[64,4096]{1,0:T(8,128)(2,1)} %param.11), channel_id=1, source_target_pairs={{0,1},{1,0},{2,3},{3,2},{4,5},{5,4},{6,7},{7,6},{8,9},{9,8},{10,11... | collective-permute-start | bytes 1572872 | tf_op jit(solution)/shard_map/ppermute | solution.py:122
  19.9 8.7 %collective-permute-done = bf16[64,4096]{1,0:T(8,128)(2,1)S(1)} collective-permute-done((bf16[64,4096]{1,0:T(8,128)(2,1)}, bf16[64,4096]{1,0:T(8,128)(2,1)S(1)}, u32[]{:S(2)}, u32[]{:S(2)}) %collective-permute-start) | collective-permute-done | bytes 524320 | tf_op jit(solution)/shard_map/ppermute | solution.py:122
  28.6 5.1 %collective-permute-start.3 = (bf16[64,4096]{1,0:T(8,128)(2,1)S(1)}, bf16[64,4096]{1,0:T(8,128)(2,1)}, u32[]{:S(2)}, u32[]{:S(2)}) collective-permute-start(bf16[64,4096]{1,0:T(8,128)(2,1)S(1)} %collective-permute-done), channel_id=1, source_target_pairs={{0,6},{2,0},{4,2},{1,7},{3,1},{5,3},{8,14},{10,8},{12,10},{9,15},{... | collective-permute-start | bytes 1572872 | tf_op jit(solution)/shard_map/ppermute | solution.py:201
  33.6 3.0 %collective-permute-start.2 = (bf16[64,4096]{1,0:T(8,128)(2,1)S(1)}, bf16[64,4096]{1,0:T(8,128)(2,1)}, u32[]{:S(2)}, u32[]{:S(2)}) collective-permute-start(bf16[64,4096]{1,0:T(8,128)(2,1)S(1)} %collective-permute-done), channel_id=1, source_target_pairs={{0,4},{2,6},{4,0},{1,5},{3,7},{5,1},{8,12},{10,14},{12,8},{9,13},{... | collective-permute-start | bytes 1572872 | tf_op jit(solution)/shard_map/ppermute | solution.py:201
  36.7 2.3 collective-permute-start.1
  39.0 16.9 %all-gather.3.cloned.1.call-done = bf16[256,4096]{1,0:T(8,128)(2,1)} async-done(((bf16[64,4096]{1,0:T(8,128)(2,1)}), bf16[256,4096]{1,0:T(8,128)(2,1)}) %all-gather.3.cloned.1.call-update) | async-done | bytes 2097168 | tf_op jit(solution)/shard_map/all_gather | solution.py:197
  55.9 1.5 slice_dynamic-update-slice_fusion
  57.5 7.2 %collective-permute-done.1 = bf16[64,4096]{1,0:T(8,128)(2,1)} collective-permute-done((bf16[64,4096]{1,0:T(8,128)(2,1)S(1)}, bf16[64,4096]{1,0:T(8,128)(2,1)}, u32[]{:S(2)}, u32[]{:S(2)}) %collective-permute-start.1) | collective-permute-done | bytes 524320 | tf_op jit(solution)/shard_map/ppermute | solution.py:201
  68.6 1.1 fusion.3
  69.8 2.1 fusion.6
  71.9 1.8 fusion.10
  73.7 1.3 fusion.62
  75.3 1.3 fusion.61
  77.1 2.1 fusion.60
  79.3 2.1 fusion.9
  81.4 2.7 %convolution_convert_fusion = bf16[328,4096]{1,0:T(8,128)(2,1)} fusion(bf16[256,4096]{1,0:T(8,128)(2,1)S(1)} %copy-done, s32[328]{0:T(512)S(1)} %get-tuple-element.8, bf16[2,56,8,128]{3,2,1,0:T(8,128)(2,1)S(1)} %fusion.9), kind=kOutput, calls=%fused_computation.10 | convolution fusion | flops 764675584 | bytes 5014816 | tf_op jit(solution)/shard_map/dot_general | solution.py:248
  84.2 2.8 %constant_dynamic-slice_fusion.2 = (bf16[328,1024]{1,0:T(8,128)(2,1)}, bf16[328,1024]{1,0:T(8,128)(2,1)}, bf16[328,1024]{1,0:T(8,128)(2,1)S(1)}) fusion(bf16[328,4096]{1,0:T(8,128)(2,1)} %convolution_convert_fusion, s32[]{:T(128)S(6)} %select_n.289, s32[]{:T(128)S(6)} %select_n.293, s32[]{:T(128)S(6)} %select_n.291), kind=kLoop, calls=%fused_computation.115 | loop fusion | bytes 4030476 | tf_op jit(solution)/shard_map/dynamic_slice | solution.py:270
  87.0 2.3 collective-permute-start.4
  89.3 1.6 collective-permute-start.6
  91.0 1.8 collective-permute-start.5
  94.6 1.4 fusion.8
  97.0 10.6 %all-to-all-start = ((bf16[32,48,128]{2,1,0:T(8,128)(2,1)}), bf16[32,48,128]{2,1,0:T(8,128)(2,1)}, u32[]{:S(2)}, u32[]{:S(2)}) async-start(bf16[32,48,128]{2,1,0:T(8,128)(2,1)} %bitcast.2), calls=%async_computation | async-start | bytes 786432 | tf_op jit(solution)/shard_map/all_to_all | solution.py:146
  107.7 13.3 %collective-permute-done.5 = bf16[328,1024]{1,0:T(8,128)(2,1)} collective-permute-done((bf16[328,1024]{1,0:T(8,128)(2,1)S(1)}, bf16[328,1024]{1,0:T(8,128)(2,1)}, u32[]{:S(2)}, u32[]{:S(2)}) %collective-permute-start.5) | collective-permute-done | bytes 671776 | tf_op jit(solution)/shard_map/ppermute | solution.py:273
  121.0 2.2 add_convert_fusion
  126.5 10.3 %all-to-all-start.1 = ((bf16[32,48,128]{2,1,0:T(8,128)(2,1)}), bf16[32,48,128]{2,1,0:T(8,128)(2,1)S(1)}, u32[]{:S(2)}, u32[]{:S(2)}) async-start(bf16[32,48,128]{2,1,0:T(8,128)(2,1)} %bitcast.13), calls=%async_computation.1 | async-start | bytes 786432 | tf_op jit(solution)/shard_map/all_to_all | solution.py:146
  136.9 4.8 %collective-permute-start.7 = (bf16[324,512]{1,0:T(8,128)(2,1)S(1)}, bf16[324,512]{1,0:T(8,128)(2,1)S(1)}, u32[]{:S(2)}, u32[]{:S(2)}) collective-permute-start(bf16[324,512]{1,0:T(8,128)(2,1)S(1)} %get-tuple-element.13), channel_id=1, source_target_pairs={{0,1},{1,0},{2,3},{3,2},{4,5},{5,4},{6,7},{7,6},{8,9},{9,8},{10,11... | collective-permute-start | bytes 995336 | tf_op jit(solution)/shard_map/ppermute | solution.py:122
  141.7 18.5 %collective-permute-done.7 = bf16[324,512]{1,0:T(8,128)(2,1)S(1)} collective-permute-done((bf16[324,512]{1,0:T(8,128)(2,1)S(1)}, bf16[324,512]{1,0:T(8,128)(2,1)S(1)}, u32[]{:S(2)}, u32[]{:S(2)}) %collective-permute-start.7) | collective-permute-done | bytes 331808 | tf_op jit(solution)/shard_map/ppermute | solution.py:122
  161.3 4.0 %all-to-all-done.1 = bf16[32,48,128]{2,1,0:T(8,128)(2,1)S(1)} async-done(((bf16[32,48,128]{2,1,0:T(8,128)(2,1)}), bf16[32,48,128]{2,1,0:T(8,128)(2,1)S(1)}, u32[]{:S(2)}, u32[]{:S(2)}) %all-to-all-start.1) | async-done | bytes 393248 | tf_op jit(solution)/shard_map/all_to_all | solution.py:146
  165.3 7.2 %all-to-all-start.2 = ((bf16[32,48,128]{2,1,0:T(8,128)(2,1)}), bf16[32,48,128]{2,1,0:T(8,128)(2,1)S(1)}, u32[]{:S(2)}, u32[]{:S(2)}) async-start(bf16[32,48,128]{2,1,0:T(8,128)(2,1)} %bitcast.15), calls=%async_computation.2 | async-start | bytes 786432 | tf_op jit(solution)/shard_map/all_to_all | solution.py:146
  172.7 38.6 %gather_fusion = f32[6144]{0:T(1024)S(1)} fusion(f32[512]{0:T(512)S(1)} %copy-done.1, s32[6144]{0:T(1024)S(1)} %broadcast_clamp_fusion), kind=kCustom, calls=%fused_computation | custom fusion | bytes 73728 | tf_op jit(solution)/shard_map/jit(_take)/gather | solution.py:285
  211.3 1.2 add_convert_fusion.1
  212.8 21.5 %all_to_all.20 = bf16[32,48,128]{2,1,0:T(8,128)(2,1)S(1)} all-to-all(bf16[32,48,128]{2,1,0:T(8,128)(2,1)S(1)} %fusion.19), channel_id=1, replica_groups=mesh['x'=4,'zl'=4,'c'=2,'y'=4,'zh'=2] {'x','zl','c'}, dimensions={0} | all-to-all | bytes 786432 | tf_op jit(solution)/shard_map/all_to_all | solution.py:151
  (80 shorter events, 17.3 us)
Async XLA Ops:
  6.5 74.9 %copy-start = (bf16[256,4096]{1,0:T(8,128)(2,1)S(1)}, bf16[256,4096]{1,0:T(8,128)(2,1)}, u32[]{:S(2)}) copy-start(bf16[256,4096]{1,0:T(8,128)(2,1)} %param.17) | copy-start | bytes 6291460
  6.5 49.4 %all-gather.3.cloned.1.call-start = ((), (), s32[]{:S(2)}) async-start(), calls=%async_computation.4 | async-start | bytes 2621440 | tf_op jit(solution)/shard_map/all_gather | solution.py:197
  7.3 21.3 %collective-permute-start = (bf16[64,4096]{1,0:T(8,128)(2,1)}, bf16[64,4096]{1,0:T(8,128)(2,1)S(1)}, u32[]{:S(2)}, u32[]{:S(2)}) collective-permute-start(bf16[64,4096]{1,0:T(8,128)(2,1)} %param.11), channel_id=1, source_target_pairs={{0,1},{1,0},{2,3},{3,2},{4,5},{5,4},{6,7},{7,6},{8,9},{9,8},{10,11... | collective-permute-start | bytes 1572872 | tf_op jit(solution)/shard_map/ppermute | solution.py:122
  28.6 38.3 %collective-permute-start.3 = (bf16[64,4096]{1,0:T(8,128)(2,1)S(1)}, bf16[64,4096]{1,0:T(8,128)(2,1)}, u32[]{:S(2)}, u32[]{:S(2)}) collective-permute-start(bf16[64,4096]{1,0:T(8,128)(2,1)S(1)} %collective-permute-done), channel_id=1, source_target_pairs={{0,6},{2,0},{4,2},{1,7},{3,1},{5,3},{8,14},{10,8},{12,10},{9,15},{... | collective-permute-start | bytes 1572872 | tf_op jit(solution)/shard_map/ppermute | solution.py:201
  33.6 32.1 %collective-permute-start.2 = (bf16[64,4096]{1,0:T(8,128)(2,1)S(1)}, bf16[64,4096]{1,0:T(8,128)(2,1)}, u32[]{:S(2)}, u32[]{:S(2)}) collective-permute-start(bf16[64,4096]{1,0:T(8,128)(2,1)S(1)} %collective-permute-done), channel_id=1, source_target_pairs={{0,4},{2,6},{4,0},{1,5},{3,7},{5,1},{8,12},{10,14},{12,8},{9,13},{... | collective-permute-start | bytes 1572872 | tf_op jit(solution)/shard_map/ppermute | solution.py:201
  36.7 28.0 %collective-permute-start.1 = (bf16[64,4096]{1,0:T(8,128)(2,1)S(1)}, bf16[64,4096]{1,0:T(8,128)(2,1)}, u32[]{:S(2)}, u32[]{:S(2)}) collective-permute-start(bf16[64,4096]{1,0:T(8,128)(2,1)S(1)} %collective-permute-done), channel_id=1, source_target_pairs={{0,2},{2,4},{4,6},{1,3},{3,5},{5,7},{8,10},{10,12},{12,14},{9,11},... | collective-permute-start | bytes 1572872 | tf_op jit(solution)/shard_map/ppermute | solution.py:201
  68.0 1.8 copy-start.2
  68.0 1.8 copy-start.3
  68.0 1.8 copy-start.4
  69.8 2.1 copy-start.6
  71.9 1.8 copy-start.7
  73.7 1.6 copy-start.8
  87.0 20.7 %collective-permute-start.4 = (bf16[328,1024]{1,0:T(8,128)(2,1)}, bf16[328,1024]{1,0:T(8,128)(2,1)}, u32[]{:S(2)}, u32[]{:S(2)}) collective-permute-start(bf16[328,1024]{1,0:T(8,128)(2,1)} %get-tuple-element.9), channel_id=1, source_target_pairs={{0,2},{2,4},{4,6},{6,0},{1,3},{3,5},{5,7},{7,1},{8,10},{10,12},{12... | collective-permute-start | bytes 2015240 | tf_op jit(solution)/shard_map/ppermute | solution.py:273
  89.3 18.3 %collective-permute-start.6 = (bf16[328,1024]{1,0:T(8,128)(2,1)}, bf16[328,1024]{1,0:T(8,128)(2,1)}, u32[]{:S(2)}, u32[]{:S(2)}) collective-permute-start(bf16[328,1024]{1,0:T(8,128)(2,1)} %get-tuple-element.10), channel_id=1, source_target_pairs={{0,6},{2,0},{4,2},{6,4},{1,7},{3,1},{5,3},{7,5},{8,14},{10,8},{12,... | collective-permute-start | bytes 2015240 | tf_op jit(solution)/shard_map/ppermute | solution.py:273
  91.0 30.0 %collective-permute-start.5 = (bf16[328,1024]{1,0:T(8,128)(2,1)S(1)}, bf16[328,1024]{1,0:T(8,128)(2,1)}, u32[]{:S(2)}, u32[]{:S(2)}) collective-permute-start(bf16[328,1024]{1,0:T(8,128)(2,1)S(1)} %get-tuple-element.11), channel_id=1, source_target_pairs={{0,4},{2,6},{4,0},{6,2},{1,5},{3,7},{5,1},{7,3},{8,12},{10,14},{12... | collective-permute-start | bytes 2015240 | tf_op jit(solution)/shard_map/ppermute | solution.py:273
  97.0 29.5 %all-to-all-start = ((bf16[32,48,128]{2,1,0:T(8,128)(2,1)}), bf16[32,48,128]{2,1,0:T(8,128)(2,1)}, u32[]{:S(2)}, u32[]{:S(2)}) async-start(bf16[32,48,128]{2,1,0:T(8,128)(2,1)} %bitcast.2), calls=%async_computation | async-start | bytes 786432 | tf_op jit(solution)/shard_map/all_to_all | solution.py:146
  124.5 48.1 %copy-start.5 = (s32[32,1]{0,1:T(1,128)S(1)}, s32[32,1]{0,1:T(1,128)}, u32[]{:S(2)}) copy-start(s32[32,1]{0,1:T(1,128)} %param.21) | copy-start | bytes 388
  124.5 48.2 %copy-start.1 = (f32[512]{0:T(512)S(1)}, f32[512]{0:T(512)}, u32[]{:S(2)}) copy-start(f32[512]{0:T(512)} %param.18) | copy-start | bytes 6148
  126.5 38.7 %all-to-all-start.1 = ((bf16[32,48,128]{2,1,0:T(8,128)(2,1)}), bf16[32,48,128]{2,1,0:T(8,128)(2,1)S(1)}, u32[]{:S(2)}, u32[]{:S(2)}) async-start(bf16[32,48,128]{2,1,0:T(8,128)(2,1)} %bitcast.13), calls=%async_computation.1 | async-start | bytes 786432 | tf_op jit(solution)/shard_map/all_to_all | solution.py:146
  136.9 23.3 %collective-permute-start.7 = (bf16[324,512]{1,0:T(8,128)(2,1)S(1)}, bf16[324,512]{1,0:T(8,128)(2,1)S(1)}, u32[]{:S(2)}, u32[]{:S(2)}) collective-permute-start(bf16[324,512]{1,0:T(8,128)(2,1)S(1)} %get-tuple-element.13), channel_id=1, source_target_pairs={{0,1},{1,0},{2,3},{3,2},{4,5},{5,4},{6,7},{7,6},{8,9},{9,8},{10,11... | collective-permute-start | bytes 995336 | tf_op jit(solution)/shard_map/ppermute | solution.py:122
  165.3 46.1 %all-to-all-start.2 = ((bf16[32,48,128]{2,1,0:T(8,128)(2,1)}), bf16[32,48,128]{2,1,0:T(8,128)(2,1)S(1)}, u32[]{:S(2)}, u32[]{:S(2)}) async-start(bf16[32,48,128]{2,1,0:T(8,128)(2,1)} %bitcast.15), calls=%async_computation.2 | async-start | bytes 786432 | tf_op jit(solution)/shard_map/all_to_all | solution.py:146
Sparse Core Ops, SparseCore 0:
  9.1 46.7 all-gather.2

commit v6 on v4

--- a/solution.py
+++ b/solution.py
@@ -178,24 +178,26 @@
     zh = lax.axis_index("zh")
     y_index = lax.axis_index("y")
     y_count = lax.axis_size("y")
-    own_blocks = lax.all_gather(stream_rows, "y", axis=0, tiled=False)
     partner = swap_pair(stream_rows)
     live_blocks = -(-LIVE_ROWS // (2 * stream_rows.shape[0]))
-    candidates = [partner] + [
-        lax.ppermute(
-            partner, "y", [(src, (src + by) % y_count) for src in range(live_blocks)]
-        )
-        for by in range(1, y_count)
-    ]
+
+    def spread(rows_in):
+        return [rows_in] + [
+            lax.ppermute(
+                rows_in, "y", [(src, (src + by) % y_count) for src in range(live_blocks)]
+            )
+            for by in range(1, y_count)
+        ]
+
+    own_candidates = spread(stream_rows)
+    candidates = spread(partner)
     block = stream_rows.shape[0]
     in_block = jnp.arange(block, dtype=jnp.int32)
-    own_ids = (2 * jnp.arange(live_blocks, dtype=jnp.int32)[:, None] + zh) * block + in_block
     from_y = (y_index - jnp.arange(y_count, dtype=jnp.int32)) % y_count
+    own_ids = (2 * from_y[:, None] + zh) * block + in_block
     partner_ids = (2 * from_y[:, None] + 1 - zh) * block + in_block
     row_ids = jnp.concatenate([own_ids.reshape(-1), partner_ids.reshape(-1)])
-    live_rows = jnp.concatenate(
-        [own_blocks[:live_blocks].reshape(-1, stream_rows.shape[1])] + candidates, axis=0
-    )
+    live_rows = jnp.concatenate(own_candidates + candidates, axis=0)
     row_count = row_ids.shape[0]
     normed = layer_norm(live_rows, ln_gain, ln_bias)
 

time: 197 us -> 190 us (0.964)
  between operations: 15.3 us -> 1.89 us
  waiting for transfers between devices: 85 us -> 75.6 us
  starting transfers between devices: 42.7 us -> 50.1 us
  local copies, waits for them, and re-layouts: 12.3 us -> 18.9 us
  other arithmetic: 10.4 us -> 13 us
    all_gather x1 -> x0, waiting for transfers between devices: 16.9 us -> none  [body(): own_blocks = lax.all_gather(stream_rows, 'y', axis=0, tiled=False)]
    ppermute x3 -> x6, starting transfers between devices: 10.4 us -> 18.6 us  [spread(): lax.ppermute(rows_in, 'y', [(src, (src + by) % y_count) for src in range(...]
    unnamed x24 -> x28, local copies, waits for them, and re-layouts: 4.9 us -> 11.7 us
    ppermute x3 -> x6, waiting for transfers between devices: 7.23 us -> 11.3 us  [spread(): lax.ppermute(rows_in, 'y', [(src, (src + by) % y_count) for src in range(...]
    ppermute x3, waiting for transfers between devices: 28.2 us -> 31.8 us  [body(): lax.ppermute(chunk, 'y', [(src, (src + by) % y_count) for src in range(y_...]
    all_to_all x1, starting transfers between devices: 17.4 us -> 20.4 us  [shift_by_exchange(): lax.all_to_all(flat.reshape(count, rows, lanes), DP_AXES, 0, 0, tiled=True)]
    reshape x2 -> x0, matrix products: 2.64 us -> none  [the longest x1 1.32 us: body(): projected[:, head_cols:2 * head_cols].reshape(row_count, local_heads, HEAD)]
    dot_general x0 -> x2, matrix products: none -> 2.58 us  [the longest x1 1.29 us: body(): jnp.dot(normed, w_q, preferred_element_type=jnp.float32)]
  transfers between devices with their start and end apart: 10 -> 12, of which waited for: 7 -> 7; matrix products, arithmetic and copies ran while one was open for 4% -> 7% of each run, Pallas kernels for 0% -> 0%
where the time goes in v6:
time: 190 us; the launch traced here: 189 us
  waiting for transfers between devices  75.6 us (40%)
  starting transfers between devices  50.1 us (26%)
  local copies, waits for them, and re-layouts  18.9 us (10%)
  blocking collectives  17.5 us (9%)
  other arithmetic  13 us (7%)
  matrix products  12.3 us (6%)
    ppermute x3, waiting for transfers between devices, body(): lax.ppermute(chunk, 'y', [(src, (src + by) % y_count) for src in range(y_...  31.8 us
    all_to_all x1, starting transfers between devices, shift_by_exchange(): lax.all_to_all(flat.reshape(count, rows, lanes), DP_AXES, 0, 0, tiled=True)  20.4 us
    ppermute x6, starting transfers between devices, spread(): lax.ppermute(rows_in, 'y', [(src, (src + by) % y_count) for src in range(...  18.6 us
    ppermute x2, waiting for transfers between devices, swap_pair(): return lax.ppermute(array, 'zh', [(0, 1), (1, 0)])  18.5 us
    all_to_all x1, blocking collectives, shift_by_exchange(): back = lax.all_to_all(rolled, DP_AXES, 0, 0, tiled=True)  17.5 us
    all_to_all x1, waiting for transfers between devices, shift_by_exchange(): lax.all_to_all(flat.reshape(count, rows, lanes), DP_AXES, 0, 0, tiled=True)  13.9 us
    unnamed x28, local copies, waits for them, and re-layouts  11.7 us
    ppermute x6, waiting for transfers between devices, spread(): lax.ppermute(rows_in, 'y', [(src, (src + by) % y_count) for src in range(...  11.3 us
  transfers between devices with their start and end apart: 12, of which 7 were waited for; matrix products, arithmetic and copies ran while one was open for 7% of the time, Pallas kernels for 0%

profile of v6, /device:TPU:1, one launch (start us, length us, event | category | flops | bytes accessed | tf_op | source)
XLA Modules:
  0.0 189.3 jit_solution(1447164904348558319)
XLA Ops:
  0.0 5.0 %collective-permute-start = (bf16[64,4096]{1,0:T(8,128)(2,1)}, bf16[64,4096]{1,0:T(8,128)(2,1)}, u32[]{:S(2)}, u32[]{:S(2)}) collective-permute-start(bf16[64,4096]{1,0:T(8,128)(2,1)} %param.11), channel_id=1, source_target_pairs={{0,2},{2,4},{4,6},{1,3},{3,5},{5,7},{8,10},{10,12},{12,14},{9,11},... | collective-permute-start | bytes 1572872 | tf_op jit(solution)/shard_map/ppermute | solution.py:186
  5.0 3.7 %collective-permute-start.1 = (bf16[64,4096]{1,0:T(8,128)(2,1)}, bf16[64,4096]{1,0:T(8,128)(2,1)}, u32[]{:S(2)}, u32[]{:S(2)}) collective-permute-start(bf16[64,4096]{1,0:T(8,128)(2,1)} %param.11), channel_id=1, source_target_pairs={{0,4},{2,6},{4,0},{1,5},{3,7},{5,1},{8,12},{10,14},{12,8},{9,13},{... | collective-permute-start | bytes 1572872 | tf_op jit(solution)/shard_map/ppermute | solution.py:186
  8.7 1.9 %collective-permute-start.2 = (bf16[64,4096]{1,0:T(8,128)(2,1)}, bf16[64,4096]{1,0:T(8,128)(2,1)}, u32[]{:S(2)}, u32[]{:S(2)}) collective-permute-start(bf16[64,4096]{1,0:T(8,128)(2,1)} %param.11), channel_id=1, source_target_pairs={{0,6},{2,0},{4,2},{1,7},{3,1},{5,3},{8,14},{10,8},{12,10},{9,15},{... | collective-permute-start | bytes 1572872 | tf_op jit(solution)/shard_map/ppermute | solution.py:186
  10.6 7.0 %collective-permute-start.3 = (bf16[64,4096]{1,0:T(8,128)(2,1)}, bf16[64,4096]{1,0:T(8,128)(2,1)S(1)}, u32[]{:S(2)}, u32[]{:S(2)}) collective-permute-start(bf16[64,4096]{1,0:T(8,128)(2,1)} %param.11), channel_id=1, source_target_pairs={{0,1},{1,0},{2,3},{3,2},{4,5},{5,4},{6,7},{7,6},{8,9},{9,8},{10,11... | collective-permute-start | bytes 1572872 | tf_op jit(solution)/shard_map/ppermute | solution.py:122
  17.6 1.9 %constant_dynamic-update-slice_fusion.8 = bf16[512,4096]{1,0:T(8,128)(2,1)} fusion(bf16[64,4096]{1,0:T(8,128)(2,1)} %param.11), kind=kLoop, calls=%fused_computation.60 | loop fusion | bytes 1048576
  24.3 6.7 %collective-permute-done.3 = bf16[64,4096]{1,0:T(8,128)(2,1)S(1)} collective-permute-done((bf16[64,4096]{1,0:T(8,128)(2,1)}, bf16[64,4096]{1,0:T(8,128)(2,1)S(1)}, u32[]{:S(2)}, u32[]{:S(2)}) %collective-permute-start.3) | collective-permute-done | bytes 524320 | tf_op jit(solution)/shard_map/ppermute | solution.py:122
  31.0 3.1 %collective-permute-start.4 = (bf16[64,4096]{1,0:T(8,128)(2,1)S(1)}, bf16[64,4096]{1,0:T(8,128)(2,1)S(1)}, u32[]{:S(2)}, u32[]{:S(2)}) collective-permute-start(bf16[64,4096]{1,0:T(8,128)(2,1)S(1)} %collective-permute-done.3), channel_id=1, source_target_pairs={{0,2},{2,4},{4,6},{1,3},{3,5},{5,7},{8,10},{10,12},{12,14},{9,11},... | collective-permute-start | bytes 1572872 | tf_op jit(solution)/shard_map/ppermute | solution.py:186
  34.1 2.8 %collective-permute-start.5 = (bf16[64,4096]{1,0:T(8,128)(2,1)S(1)}, bf16[64,4096]{1,0:T(8,128)(2,1)S(1)}, u32[]{:S(2)}, u32[]{:S(2)}) collective-permute-start(bf16[64,4096]{1,0:T(8,128)(2,1)S(1)} %collective-permute-done.3), channel_id=1, source_target_pairs={{0,4},{2,6},{4,0},{1,5},{3,7},{5,1},{8,12},{10,14},{12,8},{9,13},{... | collective-permute-start | bytes 1572872 | tf_op jit(solution)/shard_map/ppermute | solution.py:186
  36.9 2.1 %collective-permute-start.6 = (bf16[64,4096]{1,0:T(8,128)(2,1)S(1)}, bf16[64,4096]{1,0:T(8,128)(2,1)S(1)}, u32[]{:S(2)}, u32[]{:S(2)}) collective-permute-start(bf16[64,4096]{1,0:T(8,128)(2,1)S(1)} %collective-permute-done.3), channel_id=1, source_target_pairs={{0,6},{2,0},{4,2},{1,7},{3,1},{5,3},{8,14},{10,8},{12,10},{9,15},{... | collective-permute-start | bytes 1572872 | tf_op jit(solution)/shard_map/ppermute | solution.py:186
  39.0 1.9 constant_dynamic-update-slice_fusion.7
  40.9 1.9 constant_dynamic-update-slice_fusion.6
  42.8 1.9 constant_dynamic-update-slice_fusion.5
  46.4 10.1 %collective-permute-done.5 = bf16[64,4096]{1,0:T(8,128)(2,1)S(1)} collective-permute-done((bf16[64,4096]{1,0:T(8,128)(2,1)S(1)}, bf16[64,4096]{1,0:T(8,128)(2,1)S(1)}, u32[]{:S(2)}, u32[]{:S(2)}) %collective-permute-start.5) | collective-permute-done | bytes 524320 | tf_op jit(solution)/shard_map/ppermute | solution.py:186
  57.3 1.2 collective-permute-done.6
  59.4 3.0 %convert_reduce_fusion = f32[512]{0:T(512)S(1)} fusion(bf16[512,4096]{1,0:T(8,128)(2,1)} %constant_dynamic-update-slice_fusion.1), kind=kLoop, calls=%fused_computation.2 | loop fusion | flops 4193792 | bytes 4196352 | tf_op jit(solution)/shard_map/reduce_sum | solution.py:24
  62.8 1.2 fusion.3
  64.1 2.3 %fusion.6 = bf16[512,4096]{1,0:T(8,128)(2,1)S(1)} fusion(bf16[512,4096]{1,0:T(8,128)(2,1)S(1)} %copy-done.1, f32[4096]{0:T(1024)S(1)} %copy-done.3, f32[4096]{0:T(1024)S(1)} %copy-done.4, f32[512]{0:T(512)S(1)} %add_rsqrt_fusion, f32[512]{0:T(512)S(1)} %broadcast_multiply_fusion), kind=kLoop, calls=%fused_computation.8 | loop fusion | flops 12582912 | bytes 8425472 | tf_op jit(solution)/shard_map/convert_element_type | solution.py:26
  66.4 2.0 %convolution_convert_fusion.2 = bf16[512,256]{0,1:T(8,128)(2,1)} fusion(bf16[512,4096]{1,0:T(8,128)(2,1)S(1)} %fusion.6, bf16[4096,256]{1,0:T(8,128)(2,1)S(1)} %copy-done.6), kind=kOutput, calls=%fused_computation.18 | convolution fusion | flops 1073872896 | bytes 6553600 | tf_op jit(solution)/shard_map/dot_general | solution.py:208
  68.4 1.3 fusion.55
  70.0 1.3 fusion.56
  72.8 2.2 %convolution_convert_fusion.1 = bf16[2,128,512]{2,1,0:T(8,128)(2,1)S(1)} fusion(bf16[512,2,128]{0,2,1:T(8,128)(2,1)} %bitcast.61, f32[2,512]{1,0:T(2,128)S(1)} %fusion.54, pred[512,512]{0,1:T(8,128)(4,1)S(1)} %broadcast_compare_fusion, bf16[512,2,128]{0,2,1:T(8,128)(2,1)S(1)} %get-tuple-element.15, bf16[512,2,128]{0,2,1:T(8,128)(2,1)S(1)} %get-tuple-element.14), kind=kOutput, calls=%fused_computation.17 | convolution fusion | flops 271189504 | bytes 1314816 | tf_op jit(solution)/shard_map/hqk,khd->qhd/dot_general | solution.py:107
  75.0 2.8 %convolution_convert_fusion = bf16[328,4096]{1,0:T(8,128)(2,1)} fusion(bf16[256,4096]{1,0:T(8,128)(2,1)S(1)} %copy-done, bf16[512,256]{0,1:T(8,128)(2,1)S(1)} %bitcast.57, s32[328]{0:T(512)S(1)} %get-tuple-element.8), kind=kOutput, calls=%fused_computation.9 | convolution fusion | flops 775444480 | bytes 5047584 | tf_op jit(solution)/shard_map/dot_general | solution.py:234
  77.8 2.6 %constant_dynamic-slice_fusion.2 = (bf16[328,1024]{1,0:T(8,128)(2,1)S(1)}, bf16[328,1024]{1,0:T(8,128)(2,1)}, bf16[328,1024]{1,0:T(8,128)(2,1)S(1)}) fusion(bf16[328,4096]{1,0:T(8,128)(2,1)} %convolution_convert_fusion, s32[]{:T(128)S(6)} %select_n.227, s32[]{:T(128)S(6)} %select_n.231, s32[]{:T(128)S(6)} %select_n.229), kind=kLoop, calls=%fused_computation.99 | loop fusion | bytes 4030476 | tf_op jit(solution)/shard_map/dynamic_slice | solution.py:254
  80.4 3.4 %collective-permute-start.9 = (bf16[328,1024]{1,0:T(8,128)(2,1)}, bf16[328,1024]{1,0:T(8,128)(2,1)}, u32[]{:S(2)}, u32[]{:S(2)}) collective-permute-start(bf16[328,1024]{1,0:T(8,128)(2,1)} %get-tuple-element.10), channel_id=1, source_target_pairs={{0,6},{2,0},{4,2},{6,4},{1,7},{3,1},{5,3},{7,5},{8,14},{10,8},{12,... | collective-permute-start | bytes 2015240 | tf_op jit(solution)/shard_map/ppermute | solution.py:257
  84.4 27.9 %collective-permute-done.9 = bf16[328,1024]{1,0:T(8,128)(2,1)} collective-permute-done((bf16[328,1024]{1,0:T(8,128)(2,1)}, bf16[328,1024]{1,0:T(8,128)(2,1)}, u32[]{:S(2)}, u32[]{:S(2)}) %collective-permute-start.9) | collective-permute-done | bytes 671776 | tf_op jit(solution)/shard_map/ppermute | solution.py:257
  112.4 3.9 %collective-permute-done.7 = bf16[328,1024]{1,0:T(8,128)(2,1)} collective-permute-done((bf16[328,1024]{1,0:T(8,128)(2,1)S(1)}, bf16[328,1024]{1,0:T(8,128)(2,1)}, u32[]{:S(2)}, u32[]{:S(2)}) %collective-permute-start.7) | collective-permute-done | bytes 671776 | tf_op jit(solution)/shard_map/ppermute | solution.py:257
  116.3 2.2 %add_convert_fusion = bf16[324,1024]{1,0:T(8,128)(2,1)S(1)} fusion(bf16[328,1024]{1,0:T(8,128)(2,1)} %collective-permute-done.9, bf16[328,1024]{1,0:T(8,128)(2,1)} %collective-permute-done.8, bf16[328,1024]{1,0:T(8,128)(2,1)} %collective-permute-done.7, bf16[328,4096]{1,0:T(8,128)(2,1)} %convolution_convert_fusion, s32[]{:T(128)S(6)} %select_n.225), kind=kLoop, calls=%fused_computation.14 | loop fusion | flops 2654208 | bytes 3317764 | tf_op jit(solution)/shard_map/convert_element_type | solution.py:259
  121.7 11.8 %collective-permute-done.10 = bf16[324,512]{1,0:T(8,128)(2,1)} collective-permute-done((bf16[324,512]{1,0:T(8,128)(2,1)S(1)}, bf16[324,512]{1,0:T(8,128)(2,1)}, u32[]{:S(2)}, u32[]{:S(2)}) %collective-permute-start.10) | collective-permute-done | bytes 331808 | tf_op jit(solution)/shard_map/ppermute | solution.py:122
  133.5 1.8 fusion.9
  136.3 20.4 %all-to-all-start = ((bf16[32,48,128]{2,1,0:T(8,128)(2,1)}), bf16[32,48,128]{2,1,0:T(8,128)(2,1)S(1)}, u32[]{:S(2)}, u32[]{:S(2)}) async-start(bf16[32,48,128]{2,1,0:T(8,128)(2,1)} %bitcast.14), calls=%async_computation | async-start | bytes 786432 | tf_op jit(solution)/shard_map/all_to_all | solution.py:145
  156.8 13.9 %all-to-all-done = bf16[32,48,128]{2,1,0:T(8,128)(2,1)S(1)} async-done(((bf16[32,48,128]{2,1,0:T(8,128)(2,1)}), bf16[32,48,128]{2,1,0:T(8,128)(2,1)S(1)}, u32[]{:S(2)}, u32[]{:S(2)}) %all-to-all-start) | async-done | bytes 393248 | tf_op jit(solution)/shard_map/all_to_all | solution.py:145
  170.9 17.5 %all_to_all.10 = bf16[32,48,128]{2,1,0:T(8,128)(2,1)S(1)} all-to-all(bf16[32,48,128]{2,1,0:T(8,128)(2,1)S(1)} %fusion.19), channel_id=1, replica_groups=mesh['x'=4,'zl'=4,'c'=2,'y'=4,'zh'=2] {'x','zl','c'}, dimensions={0} | all-to-all | bytes 786432 | tf_op jit(solution)/shard_map/all_to_all | solution.py:147
  (73 shorter events, 14.7 us)
Async XLA Ops:
  0.0 75.0 %copy-start = (bf16[256,4096]{1,0:T(8,128)(2,1)S(1)}, bf16[256,4096]{1,0:T(8,128)(2,1)}, u32[]{:S(2)}) copy-start(bf16[256,4096]{1,0:T(8,128)(2,1)} %param.17) | copy-start | bytes 6291460
  0.0 36.9 %collective-permute-start = (bf16[64,4096]{1,0:T(8,128)(2,1)}, bf16[64,4096]{1,0:T(8,128)(2,1)}, u32[]{:S(2)}, u32[]{:S(2)}) collective-permute-start(bf16[64,4096]{1,0:T(8,128)(2,1)} %param.11), channel_id=1, source_target_pairs={{0,2},{2,4},{4,6},{1,3},{3,5},{5,7},{8,10},{10,12},{12,14},{9,11},... | collective-permute-start | bytes 1572872 | tf_op jit(solution)/shard_map/ppermute | solution.py:186
  5.0 35.9 %collective-permute-start.1 = (bf16[64,4096]{1,0:T(8,128)(2,1)}, bf16[64,4096]{1,0:T(8,128)(2,1)}, u32[]{:S(2)}, u32[]{:S(2)}) collective-permute-start(bf16[64,4096]{1,0:T(8,128)(2,1)} %param.11), channel_id=1, source_target_pairs={{0,4},{2,6},{4,0},{1,5},{3,7},{5,1},{8,12},{10,14},{12,8},{9,13},{... | collective-permute-start | bytes 1572872 | tf_op jit(solution)/shard_map/ppermute | solution.py:186
  8.7 34.1 %collective-permute-start.2 = (bf16[64,4096]{1,0:T(8,128)(2,1)}, bf16[64,4096]{1,0:T(8,128)(2,1)}, u32[]{:S(2)}, u32[]{:S(2)}) collective-permute-start(bf16[64,4096]{1,0:T(8,128)(2,1)} %param.11), channel_id=1, source_target_pairs={{0,6},{2,0},{4,2},{1,7},{3,1},{5,3},{8,14},{10,8},{12,10},{9,15},{... | collective-permute-start | bytes 1572872 | tf_op jit(solution)/shard_map/ppermute | solution.py:186
  10.6 20.4 %collective-permute-start.3 = (bf16[64,4096]{1,0:T(8,128)(2,1)}, bf16[64,4096]{1,0:T(8,128)(2,1)S(1)}, u32[]{:S(2)}, u32[]{:S(2)}) collective-permute-start(bf16[64,4096]{1,0:T(8,128)(2,1)} %param.11), channel_id=1, source_target_pairs={{0,1},{1,0},{2,3},{3,2},{4,5},{5,4},{6,7},{7,6},{8,9},{9,8},{10,11... | collective-permute-start | bytes 1572872 | tf_op jit(solution)/shard_map/ppermute | solution.py:122
  31.0 14.5 %collective-permute-start.4 = (bf16[64,4096]{1,0:T(8,128)(2,1)S(1)}, bf16[64,4096]{1,0:T(8,128)(2,1)S(1)}, u32[]{:S(2)}, u32[]{:S(2)}) collective-permute-start(bf16[64,4096]{1,0:T(8,128)(2,1)S(1)} %collective-permute-done.3), channel_id=1, source_target_pairs={{0,2},{2,4},{4,6},{1,3},{3,5},{5,7},{8,10},{10,12},{12,14},{9,11},... | collective-permute-start | bytes 1572872 | tf_op jit(solution)/shard_map/ppermute | solution.py:186
  34.1 22.4 %collective-permute-start.5 = (bf16[64,4096]{1,0:T(8,128)(2,1)S(1)}, bf16[64,4096]{1,0:T(8,128)(2,1)S(1)}, u32[]{:S(2)}, u32[]{:S(2)}) collective-permute-start(bf16[64,4096]{1,0:T(8,128)(2,1)S(1)} %collective-permute-done.3), channel_id=1, source_target_pairs={{0,4},{2,6},{4,0},{1,5},{3,7},{5,1},{8,12},{10,14},{12,8},{9,13},{... | collective-permute-start | bytes 1572872 | tf_op jit(solution)/shard_map/ppermute | solution.py:186
  36.9 21.6 %collective-permute-start.6 = (bf16[64,4096]{1,0:T(8,128)(2,1)S(1)}, bf16[64,4096]{1,0:T(8,128)(2,1)S(1)}, u32[]{:S(2)}, u32[]{:S(2)}) collective-permute-start(bf16[64,4096]{1,0:T(8,128)(2,1)S(1)} %collective-permute-done.3), channel_id=1, source_target_pairs={{0,6},{2,0},{4,2},{1,7},{3,1},{5,3},{8,14},{10,8},{12,10},{9,15},{... | collective-permute-start | bytes 1572872 | tf_op jit(solution)/shard_map/ppermute | solution.py:186
  59.4 3.4 %copy-start.1 = (bf16[512,4096]{1,0:T(8,128)(2,1)S(1)}, bf16[512,4096]{1,0:T(8,128)(2,1)}, u32[]{:S(2)}) copy-start(bf16[512,4096]{1,0:T(8,128)(2,1)} %constant_dynamic-update-slice_fusion.1) | copy-start | bytes 12582916
  59.4 4.7 %copy-start.3 = (f32[4096]{0:T(1024)S(1)}, f32[4096]{0:T(1024)}, u32[]{:S(2)}) copy-start(f32[4096]{0:T(1024)} %param.13) | copy-start | bytes 49156
  59.4 4.7 %copy-start.4 = (f32[4096]{0:T(1024)S(1)}, f32[4096]{0:T(1024)}, u32[]{:S(2)}) copy-start(f32[4096]{0:T(1024)} %param.12) | copy-start | bytes 49156
  64.1 2.3 %copy-start.6 = (bf16[4096,256]{1,0:T(8,128)(2,1)S(1)}, bf16[4096,256]{1,0:T(8,128)(2,1)}, u32[]{:S(2)}) copy-start(bf16[4096,256]{1,0:T(8,128)(2,1)} %param.16) | copy-start | bytes 6291460
  66.4 2.0 %copy-start.7 = (bf16[4096,256]{1,0:T(8,128)(2,1)S(1)}, bf16[4096,256]{1,0:T(8,128)(2,1)}, u32[]{:S(2)}) copy-start(bf16[4096,256]{1,0:T(8,128)(2,1)} %param.14) | copy-start | bytes 6291460
  68.4 1.6 copy-start.8
  80.4 31.9 %collective-permute-start.9 = (bf16[328,1024]{1,0:T(8,128)(2,1)}, bf16[328,1024]{1,0:T(8,128)(2,1)}, u32[]{:S(2)}, u32[]{:S(2)}) collective-permute-start(bf16[328,1024]{1,0:T(8,128)(2,1)} %get-tuple-element.10), channel_id=1, source_target_pairs={{0,6},{2,0},{4,2},{6,4},{1,7},{3,1},{5,3},{7,5},{8,14},{10,8},{12,... | collective-permute-start | bytes 2015240 | tf_op jit(solution)/shard_map/ppermute | solution.py:257
  83.8 28.5 %collective-permute-start.8 = (bf16[328,1024]{1,0:T(8,128)(2,1)S(1)}, bf16[328,1024]{1,0:T(8,128)(2,1)}, u32[]{:S(2)}, u32[]{:S(2)}) collective-permute-start(bf16[328,1024]{1,0:T(8,128)(2,1)S(1)} %get-tuple-element.11), channel_id=1, source_target_pairs={{0,4},{2,6},{4,0},{6,2},{1,5},{3,7},{5,1},{7,3},{8,12},{10,14},{12... | collective-permute-start | bytes 2015240 | tf_op jit(solution)/shard_map/ppermute | solution.py:257
  83.8 32.4 %collective-permute-start.7 = (bf16[328,1024]{1,0:T(8,128)(2,1)S(1)}, bf16[328,1024]{1,0:T(8,128)(2,1)}, u32[]{:S(2)}, u32[]{:S(2)}) collective-permute-start(bf16[328,1024]{1,0:T(8,128)(2,1)S(1)} %get-tuple-element.9), channel_id=1, source_target_pairs={{0,2},{2,4},{4,6},{6,0},{1,3},{3,5},{5,7},{7,1},{8,10},{10,12},{12... | collective-permute-start | bytes 2015240 | tf_op jit(solution)/shard_map/ppermute | solution.py:257
  84.4 49.1 %copy-start.9 = (f32[512]{0:T(512)S(1)}, f32[512]{0:T(512)}, u32[]{:S(2)}) copy-start(f32[512]{0:T(512)} %param.18) | copy-start | bytes 6148
  118.8 37.9 %copy-start.5 = (s32[32,1]{0,1:T(1,128)S(1)}, s32[32,1]{0,1:T(1,128)}, u32[]{:S(2)}) copy-start(s32[32,1]{0,1:T(1,128)} %param.21) | copy-start | bytes 388
  119.8 0.9 copy-start.2
  120.7 12.8 %collective-permute-start.10 = (bf16[324,512]{1,0:T(8,128)(2,1)S(1)}, bf16[324,512]{1,0:T(8,128)(2,1)}, u32[]{:S(2)}, u32[]{:S(2)}) collective-permute-start(bf16[324,512]{1,0:T(8,128)(2,1)S(1)} %select_bitcast_fusion), channel_id=1, source_target_pairs={{0,1},{1,0},{2,3},{3,2},{4,5},{5,4},{6,7},{7,6},{8,9},{9,8},{10,11... | collective-permute-start | bytes 995336 | tf_op jit(solution)/shard_map/ppermute | solution.py:122
  136.3 34.5 %all-to-all-start = ((bf16[32,48,128]{2,1,0:T(8,128)(2,1)}), bf16[32,48,128]{2,1,0:T(8,128)(2,1)S(1)}, u32[]{:S(2)}, u32[]{:S(2)}) async-start(bf16[32,48,128]{2,1,0:T(8,128)(2,1)} %bitcast.14), calls=%async_computation | async-start | bytes 786432 | tf_op jit(solution)/shard_map/all_to_all | solution.py:145

commit v7 on v6

--- a/solution.py
+++ b/solution.py
@@ -11,7 +11,7 @@
 EXTRA = 5
 CAP = 81
 LIVE_ROWS = 336
-MERGE_PAD = 328
+MERGE_PAD = 324
 
 norm_eps = 1e-06
 

time: 190 us -> 190 us (level)
  no operation moved by 1% of the time
where the time goes in v7:
time: 190 us; the launch traced here: 189 us
  waiting for transfers between devices  76.4 us (40%)
  starting transfers between devices  50.1 us (26%)
  local copies, waits for them, and re-layouts  18.8 us (10%)
  blocking collectives  17.5 us (9%)
  matrix products  12.3 us (6%)
  other arithmetic  12.2 us (6%)
    ppermute x3, waiting for transfers between devices, body(): lax.ppermute(chunk, 'y', [(src, (src + by) % y_count) for src in range(y_...  31.8 us
    all_to_all x1, starting transfers between devices, shift_by_exchange(): lax.all_to_all(flat.reshape(count, rows, lanes), DP_AXES, 0, 0, tiled=True)  20.4 us
    ppermute x2, waiting for transfers between devices, swap_pair(): return lax.ppermute(array, 'zh', [(0, 1), (1, 0)])  19.3 us
    ppermute x6, starting transfers between devices, spread(): lax.ppermute(rows_in, 'y', [(src, (src + by) % y_count) for src in range(...  18.6 us
    all_to_all x1, blocking collectives, shift_by_exchange(): back = lax.all_to_all(rolled, DP_AXES, 0, 0, tiled=True)  17.5 us
    all_to_all x1, waiting for transfers between devices, shift_by_exchange(): lax.all_to_all(flat.reshape(count, rows, lanes), DP_AXES, 0, 0, tiled=True)  13.9 us
    unnamed x28, local copies, waits for them, and re-layouts  11.7 us
    ppermute x6, waiting for transfers between devices, spread(): lax.ppermute(rows_in, 'y', [(src, (src + by) % y_count) for src in range(...  11.4 us
  transfers between devices with their start and end apart: 12, of which 7 were waited for; matrix products, arithmetic and copies ran while one was open for 7% of the time, Pallas kernels for 0%

profile of v7, /device:TPU:1, one launch (start us, length us, event | category | flops | bytes accessed | tf_op | source)
XLA Modules:
  0.0 189.0 jit_solution(1457197155290450276)
XLA Ops:
  0.0 5.0 %collective-permute-start = (bf16[64,4096]{1,0:T(8,128)(2,1)}, bf16[64,4096]{1,0:T(8,128)(2,1)}, u32[]{:S(2)}, u32[]{:S(2)}) collective-permute-start(bf16[64,4096]{1,0:T(8,128)(2,1)} %param.11), channel_id=1, source_target_pairs={{0,2},{2,4},{4,6},{1,3},{3,5},{5,7},{8,10},{10,12},{12,14},{9,11},... | collective-permute-start | bytes 1572872 | tf_op jit(solution)/shard_map/ppermute | solution.py:186
  5.0 3.7 %collective-permute-start.1 = (bf16[64,4096]{1,0:T(8,128)(2,1)}, bf16[64,4096]{1,0:T(8,128)(2,1)}, u32[]{:S(2)}, u32[]{:S(2)}) collective-permute-start(bf16[64,4096]{1,0:T(8,128)(2,1)} %param.11), channel_id=1, source_target_pairs={{0,4},{2,6},{4,0},{1,5},{3,7},{5,1},{8,12},{10,14},{12,8},{9,13},{... | collective-permute-start | bytes 1572872 | tf_op jit(solution)/shard_map/ppermute | solution.py:186
  8.7 1.9 %collective-permute-start.2 = (bf16[64,4096]{1,0:T(8,128)(2,1)}, bf16[64,4096]{1,0:T(8,128)(2,1)}, u32[]{:S(2)}, u32[]{:S(2)}) collective-permute-start(bf16[64,4096]{1,0:T(8,128)(2,1)} %param.11), channel_id=1, source_target_pairs={{0,6},{2,0},{4,2},{1,7},{3,1},{5,3},{8,14},{10,8},{12,10},{9,15},{... | collective-permute-start | bytes 1572872 | tf_op jit(solution)/shard_map/ppermute | solution.py:186
  10.6 7.0 %collective-permute-start.3 = (bf16[64,4096]{1,0:T(8,128)(2,1)}, bf16[64,4096]{1,0:T(8,128)(2,1)S(1)}, u32[]{:S(2)}, u32[]{:S(2)}) collective-permute-start(bf16[64,4096]{1,0:T(8,128)(2,1)} %param.11), channel_id=1, source_target_pairs={{0,1},{1,0},{2,3},{3,2},{4,5},{5,4},{6,7},{7,6},{8,9},{9,8},{10,11... | collective-permute-start | bytes 1572872 | tf_op jit(solution)/shard_map/ppermute | solution.py:122
  17.6 1.9 %constant_dynamic-update-slice_fusion.8 = bf16[512,4096]{1,0:T(8,128)(2,1)} fusion(bf16[64,4096]{1,0:T(8,128)(2,1)} %param.11), kind=kLoop, calls=%fused_computation.58 | loop fusion | bytes 1048576
  24.3 6.7 %collective-permute-done.3 = bf16[64,4096]{1,0:T(8,128)(2,1)S(1)} collective-permute-done((bf16[64,4096]{1,0:T(8,128)(2,1)}, bf16[64,4096]{1,0:T(8,128)(2,1)S(1)}, u32[]{:S(2)}, u32[]{:S(2)}) %collective-permute-start.3) | collective-permute-done | bytes 524320 | tf_op jit(solution)/shard_map/ppermute | solution.py:122
  31.0 3.1 %collective-permute-start.4 = (bf16[64,4096]{1,0:T(8,128)(2,1)S(1)}, bf16[64,4096]{1,0:T(8,128)(2,1)S(1)}, u32[]{:S(2)}, u32[]{:S(2)}) collective-permute-start(bf16[64,4096]{1,0:T(8,128)(2,1)S(1)} %collective-permute-done.3), channel_id=1, source_target_pairs={{0,2},{2,4},{4,6},{1,3},{3,5},{5,7},{8,10},{10,12},{12,14},{9,11},... | collective-permute-start | bytes 1572872 | tf_op jit(solution)/shard_map/ppermute | solution.py:186
  34.1 2.8 %collective-permute-start.5 = (bf16[64,4096]{1,0:T(8,128)(2,1)S(1)}, bf16[64,4096]{1,0:T(8,128)(2,1)S(1)}, u32[]{:S(2)}, u32[]{:S(2)}) collective-permute-start(bf16[64,4096]{1,0:T(8,128)(2,1)S(1)} %collective-permute-done.3), channel_id=1, source_target_pairs={{0,4},{2,6},{4,0},{1,5},{3,7},{5,1},{8,12},{10,14},{12,8},{9,13},{... | collective-permute-start | bytes 1572872 | tf_op jit(solution)/shard_map/ppermute | solution.py:186
  36.9 2.1 %collective-permute-start.6 = (bf16[64,4096]{1,0:T(8,128)(2,1)S(1)}, bf16[64,4096]{1,0:T(8,128)(2,1)S(1)}, u32[]{:S(2)}, u32[]{:S(2)}) collective-permute-start(bf16[64,4096]{1,0:T(8,128)(2,1)S(1)} %collective-permute-done.3), channel_id=1, source_target_pairs={{0,6},{2,0},{4,2},{1,7},{3,1},{5,3},{8,14},{10,8},{12,10},{9,15},{... | collective-permute-start | bytes 1572872 | tf_op jit(solution)/shard_map/ppermute | solution.py:186
  39.0 1.9 constant_dynamic-update-slice_fusion.7
  40.9 1.9 constant_dynamic-update-slice_fusion.6
  42.8 1.9 constant_dynamic-update-slice_fusion.5
  46.3 10.2 %collective-permute-done.5 = bf16[64,4096]{1,0:T(8,128)(2,1)S(1)} collective-permute-done((bf16[64,4096]{1,0:T(8,128)(2,1)S(1)}, bf16[64,4096]{1,0:T(8,128)(2,1)S(1)}, u32[]{:S(2)}, u32[]{:S(2)}) %collective-permute-start.5) | collective-permute-done | bytes 524320 | tf_op jit(solution)/shard_map/ppermute | solution.py:186
  57.3 1.2 collective-permute-done.6
  59.3 3.0 %convert_reduce_fusion = f32[512]{0:T(512)S(1)} fusion(bf16[512,4096]{1,0:T(8,128)(2,1)} %constant_dynamic-update-slice_fusion.1), kind=kLoop, calls=%fused_computation.2 | loop fusion | flops 4193792 | bytes 4196352 | tf_op jit(solution)/shard_map/reduce_sum | solution.py:24
  62.8 1.2 fusion.3
  64.0 2.3 %fusion.6 = bf16[512,4096]{1,0:T(8,128)(2,1)S(1)} fusion(bf16[512,4096]{1,0:T(8,128)(2,1)S(1)} %copy-done.1, f32[4096]{0:T(1024)S(1)} %copy-done.3, f32[4096]{0:T(1024)S(1)} %copy-done.4, f32[512]{0:T(512)S(1)} %add_rsqrt_fusion, f32[512]{0:T(512)S(1)} %broadcast_multiply_fusion), kind=kLoop, calls=%fused_computation.8 | loop fusion | flops 12582912 | bytes 8425472 | tf_op jit(solution)/shard_map/convert_element_type | solution.py:26
  66.4 2.0 %convolution_convert_fusion.2 = bf16[512,256]{0,1:T(8,128)(2,1)} fusion(bf16[512,4096]{1,0:T(8,128)(2,1)S(1)} %fusion.6, bf16[4096,256]{1,0:T(8,128)(2,1)S(1)} %copy-done.6), kind=kOutput, calls=%fused_computation.18 | convolution fusion | flops 1073872896 | bytes 6553600 | tf_op jit(solution)/shard_map/dot_general | solution.py:208
  68.4 1.3 fusion.55
  70.0 1.3 fusion.56
  72.8 2.2 %convolution_convert_fusion.1 = bf16[2,128,512]{2,1,0:T(8,128)(2,1)S(1)} fusion(bf16[512,2,128]{0,2,1:T(8,128)(2,1)} %bitcast.61, f32[2,512]{1,0:T(2,128)S(1)} %fusion.54, pred[512,512]{0,1:T(8,128)(4,1)S(1)} %broadcast_compare_fusion, bf16[512,2,128]{0,2,1:T(8,128)(2,1)S(1)} %get-tuple-element.13, bf16[512,2,128]{0,2,1:T(8,128)(2,1)S(1)} %get-tuple-element.12), kind=kOutput, calls=%fused_computation.17 | convolution fusion | flops 271189504 | bytes 1314816 | tf_op jit(solution)/shard_map/hqk,khd->qhd/dot_general | solution.py:107
  75.0 2.8 %convolution_convert_fusion = bf16[324,4096]{1,0:T(8,128)(2,1)} fusion(bf16[256,4096]{1,0:T(8,128)(2,1)S(1)} %copy-done, bf16[512,256]{0,1:T(8,128)(2,1)S(1)} %bitcast.57, s32[324]{0:T(512)S(1)} %get-tuple-element.6), kind=kOutput, calls=%fused_computation.9 | convolution fusion | flops 765987840 | bytes 5014800 | tf_op jit(solution)/shard_map/dot_general | solution.py:234
  77.8 2.6 %constant_dynamic-slice_fusion.2 = (bf16[324,1024]{1,0:T(8,128)(2,1)S(1)}, bf16[324,1024]{1,0:T(8,128)(2,1)}, bf16[324,1024]{1,0:T(8,128)(2,1)S(1)}) fusion(bf16[324,4096]{1,0:T(8,128)(2,1)} %convolution_convert_fusion, s32[]{:T(128)S(6)} %select_n.222, s32[]{:T(128)S(6)} %select_n.226, s32[]{:T(128)S(6)} %select_n.224), kind=kLoop, calls=%fused_computation.97 | loop fusion | bytes 3981324 | tf_op jit(solution)/shard_map/dynamic_slice | solution.py:254
  80.4 3.4 %collective-permute-start.9 = (bf16[324,1024]{1,0:T(8,128)(2,1)}, bf16[324,1024]{1,0:T(8,128)(2,1)}, u32[]{:S(2)}, u32[]{:S(2)}) collective-permute-start(bf16[324,1024]{1,0:T(8,128)(2,1)} %get-tuple-element.8), channel_id=1, source_target_pairs={{0,6},{2,0},{4,2},{6,4},{1,7},{3,1},{5,3},{7,5},{8,14},{10,8},{12,... | collective-permute-start | bytes 1990664 | tf_op jit(solution)/shard_map/ppermute | solution.py:257
  84.4 27.9 %collective-permute-done.9 = bf16[324,1024]{1,0:T(8,128)(2,1)} collective-permute-done((bf16[324,1024]{1,0:T(8,128)(2,1)}, bf16[324,1024]{1,0:T(8,128)(2,1)}, u32[]{:S(2)}, u32[]{:S(2)}) %collective-permute-start.9) | collective-permute-done | bytes 663584 | tf_op jit(solution)/shard_map/ppermute | solution.py:257
  112.3 3.9 %collective-permute-done.7 = bf16[324,1024]{1,0:T(8,128)(2,1)} collective-permute-done((bf16[324,1024]{1,0:T(8,128)(2,1)S(1)}, bf16[324,1024]{1,0:T(8,128)(2,1)}, u32[]{:S(2)}, u32[]{:S(2)}) %collective-permute-start.7) | collective-permute-done | bytes 663584 | tf_op jit(solution)/shard_map/ppermute | solution.py:257
  116.2 2.2 %add_convert_fusion = bf16[324,1024]{1,0:T(8,128)(2,1)S(1)} fusion(bf16[324,1024]{1,0:T(8,128)(2,1)} %collective-permute-done.9, bf16[324,1024]{1,0:T(8,128)(2,1)} %collective-permute-done.8, bf16[324,1024]{1,0:T(8,128)(2,1)} %collective-permute-done.7, bf16[324,4096]{1,0:T(8,128)(2,1)} %convolution_convert_fusion, s32[]{:T(128)S(6)} %select_n.220), kind=kLoop, calls=%fused_computation.14 | loop fusion | flops 2654208 | bytes 3317764 | tf_op jit(solution)/shard_map/convert_element_type | solution.py:259
  120.8 12.5 %collective-permute-done.10 = bf16[324,512]{1,0:T(8,128)(2,1)S(1)} collective-permute-done((bf16[324,512]{1,0:T(8,128)(2,1)S(1)}, bf16[324,512]{1,0:T(8,128)(2,1)S(1)}, u32[]{:S(2)}, u32[]{:S(2)}) %collective-permute-start.10) | collective-permute-done | bytes 331808 | tf_op jit(solution)/shard_map/ppermute | solution.py:122
  133.3 1.7 fusion.9
  136.0 20.4 %all-to-all-start = ((bf16[32,48,128]{2,1,0:T(8,128)(2,1)}), bf16[32,48,128]{2,1,0:T(8,128)(2,1)S(1)}, u32[]{:S(2)}, u32[]{:S(2)}) async-start(bf16[32,48,128]{2,1,0:T(8,128)(2,1)} %bitcast.14), calls=%async_computation | async-start | bytes 786432 | tf_op jit(solution)/shard_map/all_to_all | solution.py:145
  156.6 13.9 %all-to-all-done = bf16[32,48,128]{2,1,0:T(8,128)(2,1)S(1)} async-done(((bf16[32,48,128]{2,1,0:T(8,128)(2,1)}), bf16[32,48,128]{2,1,0:T(8,128)(2,1)S(1)}, u32[]{:S(2)}, u32[]{:S(2)}) %all-to-all-start) | async-done | bytes 393248 | tf_op jit(solution)/shard_map/all_to_all | solution.py:145
  170.7 17.5 %all_to_all.10 = bf16[32,48,128]{2,1,0:T(8,128)(2,1)S(1)} all-to-all(bf16[32,48,128]{2,1,0:T(8,128)(2,1)S(1)} %fusion.19), channel_id=1, replica_groups=mesh['x'=4,'zl'=4,'c'=2,'y'=4,'zh'=2] {'x','zl','c'}, dimensions={0} | all-to-all | bytes 786432 | tf_op jit(solution)/shard_map/all_to_all | solution.py:147
  (71 shorter events, 13.8 us)
Async XLA Ops:
  0.0 75.0 %copy-start = (bf16[256,4096]{1,0:T(8,128)(2,1)S(1)}, bf16[256,4096]{1,0:T(8,128)(2,1)}, u32[]{:S(2)}) copy-start(bf16[256,4096]{1,0:T(8,128)(2,1)} %param.17) | copy-start | bytes 6291460
  0.0 36.9 %collective-permute-start = (bf16[64,4096]{1,0:T(8,128)(2,1)}, bf16[64,4096]{1,0:T(8,128)(2,1)}, u32[]{:S(2)}, u32[]{:S(2)}) collective-permute-start(bf16[64,4096]{1,0:T(8,128)(2,1)} %param.11), channel_id=1, source_target_pairs={{0,2},{2,4},{4,6},{1,3},{3,5},{5,7},{8,10},{10,12},{12,14},{9,11},... | collective-permute-start | bytes 1572872 | tf_op jit(solution)/shard_map/ppermute | solution.py:186
  5.0 35.9 %collective-permute-start.1 = (bf16[64,4096]{1,0:T(8,128)(2,1)}, bf16[64,4096]{1,0:T(8,128)(2,1)}, u32[]{:S(2)}, u32[]{:S(2)}) collective-permute-start(bf16[64,4096]{1,0:T(8,128)(2,1)} %param.11), channel_id=1, source_target_pairs={{0,4},{2,6},{4,0},{1,5},{3,7},{5,1},{8,12},{10,14},{12,8},{9,13},{... | collective-permute-start | bytes 1572872 | tf_op jit(solution)/shard_map/ppermute | solution.py:186
  8.7 34.1 %collective-permute-start.2 = (bf16[64,4096]{1,0:T(8,128)(2,1)}, bf16[64,4096]{1,0:T(8,128)(2,1)}, u32[]{:S(2)}, u32[]{:S(2)}) collective-permute-start(bf16[64,4096]{1,0:T(8,128)(2,1)} %param.11), channel_id=1, source_target_pairs={{0,6},{2,0},{4,2},{1,7},{3,1},{5,3},{8,14},{10,8},{12,10},{9,15},{... | collective-permute-start | bytes 1572872 | tf_op jit(solution)/shard_map/ppermute | solution.py:186
  10.6 20.4 %collective-permute-start.3 = (bf16[64,4096]{1,0:T(8,128)(2,1)}, bf16[64,4096]{1,0:T(8,128)(2,1)S(1)}, u32[]{:S(2)}, u32[]{:S(2)}) collective-permute-start(bf16[64,4096]{1,0:T(8,128)(2,1)} %param.11), channel_id=1, source_target_pairs={{0,1},{1,0},{2,3},{3,2},{4,5},{5,4},{6,7},{7,6},{8,9},{9,8},{10,11... | collective-permute-start | bytes 1572872 | tf_op jit(solution)/shard_map/ppermute | solution.py:122
  31.0 14.5 %collective-permute-start.4 = (bf16[64,4096]{1,0:T(8,128)(2,1)S(1)}, bf16[64,4096]{1,0:T(8,128)(2,1)S(1)}, u32[]{:S(2)}, u32[]{:S(2)}) collective-permute-start(bf16[64,4096]{1,0:T(8,128)(2,1)S(1)} %collective-permute-done.3), channel_id=1, source_target_pairs={{0,2},{2,4},{4,6},{1,3},{3,5},{5,7},{8,10},{10,12},{12,14},{9,11},... | collective-permute-start | bytes 1572872 | tf_op jit(solution)/shard_map/ppermute | solution.py:186
  34.1 22.4 %collective-permute-start.5 = (bf16[64,4096]{1,0:T(8,128)(2,1)S(1)}, bf16[64,4096]{1,0:T(8,128)(2,1)S(1)}, u32[]{:S(2)}, u32[]{:S(2)}) collective-permute-start(bf16[64,4096]{1,0:T(8,128)(2,1)S(1)} %collective-permute-done.3), channel_id=1, source_target_pairs={{0,4},{2,6},{4,0},{1,5},{3,7},{5,1},{8,12},{10,14},{12,8},{9,13},{... | collective-permute-start | bytes 1572872 | tf_op jit(solution)/shard_map/ppermute | solution.py:186
  36.9 21.6 %collective-permute-start.6 = (bf16[64,4096]{1,0:T(8,128)(2,1)S(1)}, bf16[64,4096]{1,0:T(8,128)(2,1)S(1)}, u32[]{:S(2)}, u32[]{:S(2)}) collective-permute-start(bf16[64,4096]{1,0:T(8,128)(2,1)S(1)} %collective-permute-done.3), channel_id=1, source_target_pairs={{0,6},{2,0},{4,2},{1,7},{3,1},{5,3},{8,14},{10,8},{12,10},{9,15},{... | collective-permute-start | bytes 1572872 | tf_op jit(solution)/shard_map/ppermute | solution.py:186
  59.3 3.4 %copy-start.1 = (bf16[512,4096]{1,0:T(8,128)(2,1)S(1)}, bf16[512,4096]{1,0:T(8,128)(2,1)}, u32[]{:S(2)}) copy-start(bf16[512,4096]{1,0:T(8,128)(2,1)} %constant_dynamic-update-slice_fusion.1) | copy-start | bytes 12582916
  59.3 4.7 %copy-start.3 = (f32[4096]{0:T(1024)S(1)}, f32[4096]{0:T(1024)}, u32[]{:S(2)}) copy-start(f32[4096]{0:T(1024)} %param.13) | copy-start | bytes 49156
  59.3 4.7 %copy-start.4 = (f32[4096]{0:T(1024)S(1)}, f32[4096]{0:T(1024)}, u32[]{:S(2)}) copy-start(f32[4096]{0:T(1024)} %param.12) | copy-start | bytes 49156
  64.0 2.3 %copy-start.6 = (bf16[4096,256]{1,0:T(8,128)(2,1)S(1)}, bf16[4096,256]{1,0:T(8,128)(2,1)}, u32[]{:S(2)}) copy-start(bf16[4096,256]{1,0:T(8,128)(2,1)} %param.16) | copy-start | bytes 6291460
  66.4 2.0 %copy-start.7 = (bf16[4096,256]{1,0:T(8,128)(2,1)S(1)}, bf16[4096,256]{1,0:T(8,128)(2,1)}, u32[]{:S(2)}) copy-start(bf16[4096,256]{1,0:T(8,128)(2,1)} %param.14) | copy-start | bytes 6291460
  68.4 1.6 copy-start.8
  80.4 31.9 %collective-permute-start.9 = (bf16[324,1024]{1,0:T(8,128)(2,1)}, bf16[324,1024]{1,0:T(8,128)(2,1)}, u32[]{:S(2)}, u32[]{:S(2)}) collective-permute-start(bf16[324,1024]{1,0:T(8,128)(2,1)} %get-tuple-element.8), channel_id=1, source_target_pairs={{0,6},{2,0},{4,2},{6,4},{1,7},{3,1},{5,3},{7,5},{8,14},{10,8},{12,... | collective-permute-start | bytes 1990664 | tf_op jit(solution)/shard_map/ppermute | solution.py:257
  83.8 28.5 %collective-permute-start.8 = (bf16[324,1024]{1,0:T(8,128)(2,1)S(1)}, bf16[324,1024]{1,0:T(8,128)(2,1)}, u32[]{:S(2)}, u32[]{:S(2)}) collective-permute-start(bf16[324,1024]{1,0:T(8,128)(2,1)S(1)} %get-tuple-element.9), channel_id=1, source_target_pairs={{0,4},{2,6},{4,0},{6,2},{1,5},{3,7},{5,1},{7,3},{8,12},{10,14},{12... | collective-permute-start | bytes 1990664 | tf_op jit(solution)/shard_map/ppermute | solution.py:257
  83.8 32.4 %collective-permute-start.7 = (bf16[324,1024]{1,0:T(8,128)(2,1)S(1)}, bf16[324,1024]{1,0:T(8,128)(2,1)}, u32[]{:S(2)}, u32[]{:S(2)}) collective-permute-start(bf16[324,1024]{1,0:T(8,128)(2,1)S(1)} %get-tuple-element.7), channel_id=1, source_target_pairs={{0,2},{2,4},{4,6},{6,0},{1,3},{3,5},{5,7},{7,1},{8,10},{10,12},{12... | collective-permute-start | bytes 1990664 | tf_op jit(solution)/shard_map/ppermute | solution.py:257
  84.4 48.9 %copy-start.9 = (f32[512]{0:T(512)S(1)}, f32[512]{0:T(512)}, u32[]{:S(2)}) copy-start(f32[512]{0:T(512)} %param.18) | copy-start | bytes 6148
  118.8 37.7 %copy-start.5 = (s32[32,1]{0,1:T(1,128)S(1)}, s32[32,1]{0,1:T(1,128)}, u32[]{:S(2)}) copy-start(s32[32,1]{0,1:T(1,128)} %param.21) | copy-start | bytes 388
  119.7 0.8 copy-start.2
  120.6 12.7 %collective-permute-start.10 = (bf16[324,512]{1,0:T(8,128)(2,1)S(1)}, bf16[324,512]{1,0:T(8,128)(2,1)S(1)}, u32[]{:S(2)}, u32[]{:S(2)}) collective-permute-start(bf16[324,512]{1,0:T(8,128)(2,1)S(1)} %select_bitcast_fusion), channel_id=1, source_target_pairs={{0,1},{1,0},{2,3},{3,2},{4,5},{5,4},{6,7},{7,6},{8,9},{9,8},{10,11... | collective-permute-start | bytes 995336 | tf_op jit(solution)/shard_map/ppermute | solution.py:122
  136.0 34.5 %all-to-all-start = ((bf16[32,48,128]{2,1,0:T(8,128)(2,1)}), bf16[32,48,128]{2,1,0:T(8,128)(2,1)S(1)}, u32[]{:S(2)}, u32[]{:S(2)}) async-start(bf16[32,48,128]{2,1,0:T(8,128)(2,1)} %bitcast.14), calls=%async_computation | async-start | bytes 786432 | tf_op jit(solution)/shard_map/all_to_all | solution.py:145
